TPU v7x, 512 devices: a whole 4x4x16 slice. The times are simulated.
512 devices in a mesh: fit: 32 (over z, core), orb: 16 (over x, y).
Axes of the slice: x: 4, y: 4, z: 16, core: 2. Of those that a mesh axis runs over, the one named last changes fastest.
Arguments:
- half_ints: bfloat16 [16, 256, 768, 256], P('orb', None, 'fit'), may hold values from -6 to 6
- osv_coef: bfloat16 [16, 256, 256, 64], P('orb', 'fit'), may hold values from -0.09375 to 0.09375
- fit_blocks: int32 [16, 256, 6], P('orb', 'fit'), may hold values from 0 to 468, as said below
- partner_list: int32 [32, 16, 24], P('fit'), may hold values from 0 to 127, as said below
Outputs:
- pair_ints: bfloat16 [16, 256, 24, 4096], P('orb', 'fit')
Inputs may be any that keep to these rules, and one draw needn't show every extreme that they name: `fit_blocks`: the 6 block numbers of one orbital are distinct. `partner_list`: entry h * 8 + k names orbital k of the same column in group h. The 24 entries of one list are distinct. Of one list, at most 3 entries name orbitals of any one group, and in every list some group is named exactly 3 times.
All inputs are finite; a program needn't handle non-finite values.
Results may differ from a plain program's by a relative error of at most 0.0055.
Values may be sent and summed in bfloat16 or wider, within the bound.
No kernel may reach another device: no remote copies, remote signals or barrier semaphores. Data moves between devices by JAX's collectives and lax.ppermute only.
A program may use at most 64 MiB of HBM per device.

v0:
```python
import jax
import jax.numpy as jnp
from jax import lax
from jax.sharding import PartitionSpec as P

BLK = 128
FBLK = 6


def per_device(half_ints, osv_coef, fit_blocks, partner_list):
    local_rows = half_ints[0]
    own_ints = lax.all_to_all(local_rows, "fit", split_axis=0, concat_axis=1, tiled=True)
    osv_local = osv_coef[0]
    projected = jnp.einsum(
        "kfa,kao->kof", own_ints, osv_local, preferred_element_type=jnp.float32
    ).astype(jnp.bfloat16)
    own_blocks = fit_blocks[0]
    column_lists = partner_list[0]
    nosv_count = projected.shape[1]
    npart_count = column_lists.shape[1]
    my_group = lax.axis_index("orb")
    wanted = lax.dynamic_index_in_dim(column_lists, my_group, 0, keepdims=False)
    piece_rows = lax.all_gather(projected, "orb", axis=0, tiled=True)
    piece_blocks = lax.all_gather(own_blocks, "orb", axis=0, tiled=True)
    piece_len = piece_rows.shape[0]
    matches = wanted[:, None] == jnp.arange(piece_len, dtype=jnp.int32)[None, :]
    buffer = jnp.einsum(
        "nr,rxf->nxf", matches.astype(jnp.bfloat16), piece_rows, preferred_element_type=jnp.float32
    ).astype(jnp.bfloat16)
    blocks = jnp.sum(jnp.where(matches[:, :, None], piece_blocks[None, :, :], 0), axis=1).astype(
        jnp.int32
    )
    partner_pieces = buffer.reshape(npart_count, nosv_count, FBLK, BLK)

    def pair_block(operand):
        own_rows, own_ids = operand
        matching = (own_ids[None, :, None] == blocks[:, None, :]).astype(jnp.bfloat16)
        aligned = jnp.einsum(
            "nbc,nxcp->nxbp", matching, partner_pieces, preferred_element_type=jnp.float32
        ).astype(jnp.bfloat16)
        pair_vals = jnp.einsum(
            "abp,nxbp->nax",
            own_rows.reshape(nosv_count, FBLK, BLK),
            aligned,
            preferred_element_type=jnp.float32,
        )
        return pair_vals.astype(jnp.bfloat16).reshape(npart_count, nosv_count * nosv_count)

    result = lax.map(pair_block, (projected, own_blocks))
    return result[None]


def solution(mesh):
    return jax.shard_map(
        per_device,
        mesh=mesh,
        in_specs=(
            P("orb", None, "fit", None),
            P("orb", "fit", None, None),
            P("orb", "fit", None),
            P("fit", None, None),
        ),
        out_specs=P("orb", "fit", None, None),
        check_vma=False,
    )
```

profile of v0, /device:TPU:1, one launch (start us, length us, event | category | flops | bytes accessed | tf_op | source)
XLA Modules:
  0.0 406.4 jit_solution(8026830469797910473)
XLA Ops:
  6.5 162.5 %all_to_all.18 = bf16[256,24,256]{2,1,0:T(8,128)(2,1)S(1)} all-to-all(bf16[256,24,256]{2,1,0:T(8,128)(2,1)} %bitcast.55), channel_id=1, replica_groups=mesh['fit'=32,'orb'=16] {'fit'}, dimensions={0} | all-to-all | bytes 6291456 | tf_op jit(solution)/shard_map/all_to_all | solution.py:12
  169.2 2.0 convolution_convert_fusion
  171.4 19.8 %all-gather = s32[1,128,6]{2,0,1:T(1,128)S(1)} all-gather(s32[1,8,6]{2,0,1:T(1,128)S(1)} %copy.31), channel_id=2, replica_groups=mesh['fit'=32,'orb'=16] {'orb'}, dimensions={1}, use_global_device_ids=true | all-gather | bytes 3264 | tf_op jit(solution)/shard_map/all_gather | solution.py:24
  192.4 75.6 %all-gather.3.cloned.1.call-done = bf16[128,64,768]{2,1,0:T(8,128)(2,1)} async-done(((bf16[8,64,768]{2,1,0:T(8,128)(2,1)}), bf16[128,64,768]{2,1,0:T(8,128)(2,1)}) %all-gather.3.cloned.1.call-update) | async-done | bytes 12582928 | tf_op jit(solution)/shard_map/all_gather | solution.py:23
  268.0 18.0 %fusion.20 = bf16[24,64,768]{2,0,1:T(8,128)(2,1)S(1)} fusion(bf16[128,64,768]{2,1,0:T(8,128)(2,1)} %all-gather.3.cloned.1.call-done, s32[24]{0:T(128)S(1)} %dynamic-slice_bitcast_fusion), kind=kOutput, calls=%fused_computation.18 | convolution fusion | flops 303172608 | bytes 14942304 | tf_op jit(solution)/shard_map/nr,rxf->nxf/dot_general | solution.py:27
  286.0 1.9 copy.35
  287.9 4.8 %reshape.40 = bf16[24,64,6,128]{3,2,1,0:T(8,128)(2,1)S(1)} reshape(bf16[24,64,768]{2,1,0:T(8,128)(2,1)} %copy.35) | data formatting | bytes 4718592 | tf_op jit(solution)/shard_map/reshape | solution.py:33
  292.8 106.8 %while.10 = (s32[]{:T(128)}, bf16[8,24,4096]{2,1,0:T(8,128)(2,1)}, s32[8,6]{1,0:T(8,128)S(1)}, s32[24,6]{1,0:T(8,128)S(1)}, bf16[24,64,6,128]{3,2,1,0:T(8,128)(2,1)S(1)}, /*index=5*/bf16[8,64,768]{2,1,0:T(8,128)(2,1)}, s32[]{:T(128)}) while((s32[]{:T(128)}, bf16[8,24,4096]{2,1,0:T(8,128)(2,1)}, s32[8,6]{1,0:T(8,128)S(1)}, ...), condition=%wide.region_2.3_spmd, body=%wide.region_1.2_spmd.sunk | while | flops 166429536 | bytes 8946909 | solution.py:49
  292.8 2.7 convert_bitcast_fusion.2
  297.1 3.4 fusion.38
  300.5 1.9 copy.60
  302.5 2.0 broadcast_in_dim.45
  304.5 1.6 constant_dynamic-update-slice_fusion.2
  306.1 2.7 convert_bitcast_fusion.2
  310.5 3.4 fusion.38
  313.9 1.9 copy.60
  315.8 2.0 broadcast_in_dim.45
  317.9 1.6 constant_dynamic-update-slice_fusion.2
  319.5 2.7 convert_bitcast_fusion.2
  323.8 3.4 fusion.38
  327.3 1.9 copy.60
  329.2 2.0 broadcast_in_dim.45
  331.2 1.6 constant_dynamic-update-slice_fusion.2
  332.8 2.7 convert_bitcast_fusion.2
  337.2 3.4 fusion.38
  340.6 1.9 copy.60
  342.5 2.0 broadcast_in_dim.45
  344.6 1.6 constant_dynamic-update-slice_fusion.2
  346.2 2.7 convert_bitcast_fusion.2
  350.5 3.4 fusion.38
  354.0 1.9 copy.60
  355.9 2.0 broadcast_in_dim.45
  357.9 1.6 constant_dynamic-update-slice_fusion.2
  359.5 2.7 convert_bitcast_fusion.2
  363.9 3.4 fusion.38
  367.3 1.9 copy.60
  369.2 2.0 broadcast_in_dim.45
  371.3 1.6 constant_dynamic-update-slice_fusion.2
  372.9 2.7 convert_bitcast_fusion.2
  377.2 3.4 fusion.38
  380.7 1.9 copy.60
  382.6 2.0 broadcast_in_dim.45
  384.6 1.6 constant_dynamic-update-slice_fusion.2
  386.2 2.7 convert_bitcast_fusion.2
  390.6 3.4 fusion.38
  394.0 1.9 copy.60
  395.9 2.0 broadcast_in_dim.45
  398.0 1.6 constant_dynamic-update-slice_fusion.2
  (39 shorter events, 15.0 us)
Async XLA Ops:
  6.5 162.7 %copy-start = (bf16[1,8,256,64]{2,3,1,0:T(8,128)(2,1)S(1)}, bf16[1,8,256,64]{2,3,1,0:T(8,128)(2,1)}, u32[]{:S(2)}) copy-start(bf16[1,8,256,64]{2,3,1,0:T(8,128)(2,1)} %param.7) | copy-start | bytes 786436
  6.5 261.4 %all-gather.3.cloned.1.call-start = ((), (), s32[]{:S(2)}) async-start(), calls=%async_computation.1 | async-start | bytes 13369344 | tf_op jit(solution)/shard_map/all_gather | solution.py:23
  169.2 2.1 copy-start.1
Sparse Core Ops, SparseCore 0:
  171.4 96.5 all-gather.2
where the time goes:
time: 408 us; the launch traced here: 406 us
  blocking collectives  182 us (45%)
  waiting for transfers between devices  75.6 us (19%)
  matrix products  68.8 us (17%)
  local copies, waits for them, and re-layouts  66 us (16%)
  between operations  13.5 us (3%)
    all_to_all x1, blocking collectives, per_device(): lax.all_to_all(local_rows, 'fit', split_axis=0, concat_axis=1, tiled=True)  162 us
    all_gather x1, waiting for transfers between devices, per_device(): piece_rows = lax.all_gather(projected, 'orb', axis=0, tiled=True)  75.6 us
    dot_general x8, matrix products, pair_block(): jnp.einsum('abp,nxbp->nax', own_rows.reshape(nosv_count, FBLK, BLK), alig...  27.3 us
    dot_general x8, matrix products, pair_block(): jnp.einsum('nbc,nxcp->nxbp', matching, partner_pieces, preferred_element_...  21.5 us
    all_gather x1, blocking collectives, per_device(): piece_blocks = lax.all_gather(own_blocks, 'orb', axis=0, tiled=True)  19.8 us
    dot_general x1, matrix products, per_device(): jnp.einsum('nr,rxf->nxf', matches.astype(jnp.bfloat16), piece_rows, prefe...  18 us
    broadcast_in_dim x8, local copies, waits for them, and re-layouts, per_device(): result = lax.map(pair_block, (projected, own_blocks))  16.3 us
    convert_element_type x8, local copies, waits for them, and re-layouts, pair_block(): pair_vals.astype(jnp.bfloat16).reshape(npart_count, nosv_count * nosv_count)  15.4 us
  transfers between devices with their start and end apart: 1, of which 1 were waited for; matrix products, arithmetic and copies ran while one was open for 0% of the time, Pallas kernels for 0%

commit v1 on v0

v1 whole, which is shorter than its diff:
```python
import jax
import jax.numpy as jnp
import numpy as np
from jax import lax
from jax.sharding import Mesh, PartitionSpec as P

BLK = 128
FBLK = 6
CAP = 3
ORB_DEV = 8


def per_device(half_ints, osv_coef, fit_blocks, partner_list):
    nz = lax.axis_size("z")
    ncore = lax.axis_size("core")
    rows = half_ints[0]
    n_orb, fchunk, aod = rows.shape
    rows = rows.reshape(nz, ncore, n_orb // (nz * ncore), fchunk, aod)
    mine = lax.all_to_all(rows, "core", split_axis=1, concat_axis=3, tiled=True)
    mine = mine.reshape(nz, n_orb // (nz * ncore), ncore * fchunk, aod)
    coef = lax.all_gather(osv_coef[0], "z", axis=0, tiled=False)
    part = jnp.einsum(
        "zkfm,zkma->zkaf", mine, coef, preferred_element_type=jnp.float32
    ).astype(jnp.bfloat16)
    projected = lax.all_to_all(part, "z", split_axis=0, concat_axis=3, tiled=True)[0]
    n_loc, nosv, fd = projected.shape

    own_blocks = fit_blocks[0]
    lists = partner_list[0]
    ngroups, npart = lists.shape
    owner = lists // ORB_DEV
    sub = lists % ORB_DEV
    earlier = jnp.tril(jnp.ones((npart, npart), jnp.int32), -1)
    same = (owner[:, :, None] == owner[:, None, :]).astype(jnp.int32)
    rank = jnp.sum(same * earlier[None], axis=2)
    me = lax.axis_index("orb")
    sel = (
        (owner == me)[:, :, None, None]
        & (rank[:, :, None, None] == jnp.arange(CAP)[None, None, :, None])
        & (sub[:, :, None, None] == jnp.arange(n_loc)[None, None, None, :])
    )
    sel = jnp.sum(sel.astype(jnp.float32), axis=1).astype(jnp.bfloat16)
    code = jnp.concatenate(
        [own_blocks // 8, own_blocks % 8, jnp.zeros((n_loc, 128 - 2 * FBLK), jnp.int32)], axis=1
    ).astype(jnp.bfloat16)
    payload = jnp.concatenate([projected.reshape(n_loc, nosv * fd), code], axis=1)
    send = jnp.einsum("dsk,kv->dsv", sel, payload, preferred_element_type=jnp.float32).astype(
        jnp.bfloat16
    )
    recv = lax.all_to_all(send, "orb", split_axis=0, concat_axis=0, tiled=True)
    recv = recv.reshape(ngroups * CAP, -1)
    my_owner = lax.dynamic_index_in_dim(owner, me, 0, keepdims=False)
    my_rank = lax.dynamic_index_in_dim(rank, me, 0, keepdims=False)
    slot = my_owner * CAP + my_rank
    pick = (slot[:, None] == jnp.arange(ngroups * CAP)[None, :]).astype(jnp.bfloat16)
    partner = jnp.einsum("ns,sv->nv", pick, recv, preferred_element_type=jnp.float32)
    pcode = partner[:, nosv * fd : nosv * fd + 2 * FBLK]
    pblocks = (pcode[:, :FBLK] * 8 + pcode[:, FBLK:]).astype(jnp.int32)
    prow = partner[:, : nosv * fd].astype(jnp.bfloat16).reshape(npart, nosv, FBLK, BLK)

    match = (own_blocks[:, None, :, None] == pblocks[None, :, None, :]).astype(jnp.bfloat16)
    aligned = jnp.einsum(
        "rnbe,nxep->rnxbp", match, prow, preferred_element_type=jnp.float32
    ).astype(jnp.bfloat16)
    pair = jnp.einsum(
        "rabp,rnxbp->rnax",
        projected.reshape(n_loc, nosv, FBLK, BLK),
        aligned,
        preferred_element_type=jnp.float32,
    ).astype(jnp.bfloat16)
    return pair.reshape(1, n_loc, npart, nosv * nosv)


def solution(mesh):
    nfit = mesh.shape["fit"]
    norb = mesh.shape["orb"]
    devs = np.asarray(mesh.devices).reshape(nfit // 2, 2, norb)
    mesh3 = Mesh(devs, ("z", "core", "orb"))
    fit = ("z", "core")
    return jax.shard_map(
        per_device,
        mesh=mesh3,
        in_specs=(
            P("orb", None, fit, None),
            P("orb", fit, None, None),
            P("orb", fit, None),
            P(fit, None, None),
        ),
        out_specs=P("orb", fit, None, None),
        check_vma=False,
    )
```

time: 408 us -> 297 us (0.73)
  the two profiles are of different devices: /device:TPU:1 before, /device:TPU:92 now
where the time goes in v1:
time: 297 us
  waiting for transfers between devices  186 us (63%)
  local copies, waits for them, and re-layouts  44 us (15%)
  matrix products  31.1 us (10%)
  starting transfers between devices  15.2 us (5%)
  between operations  13.5 us (5%)
  blocking collectives  6.26 us (2%)
    all_to_all x1, waiting for transfers between devices, per_device(): recv = lax.all_to_all(send, 'orb', split_axis=0, concat_axis=0, tiled=True)  82.8 us
    all_gather x1, waiting for transfers between devices, per_device(): coef = lax.all_gather(osv_coef[0], 'z', axis=0, tiled=False)  74.2 us
    all_to_all x1, waiting for transfers between devices, per_device(): lax.all_to_all(part, 'z', split_axis=0, concat_axis=3, tiled=True)[0]  28 us
    dot_general x1, matrix products, per_device(): jnp.einsum('rabp,rnxbp->rnax', projected.reshape(n_loc, nosv, FBLK, BLK),...  12.5 us
    dot_general x1, matrix products, per_device(): jnp.einsum('rnbe,nxep->rnxbp', match, prow, preferred_element_type=jnp.fl...  9.14 us
    all_to_all x1, starting transfers between devices, per_device(): lax.all_to_all(part, 'z', split_axis=0, concat_axis=3, tiled=True)[0]  8.3 us
    reshape x1, local copies, waits for them, and re-layouts, per_device(): recv = recv.reshape(ngroups * CAP, -1)  7.27 us
    all_to_all x1, starting transfers between devices, per_device(): recv = lax.all_to_all(send, 'orb', split_axis=0, concat_axis=0, tiled=True)  6.93 us
  transfers between devices with their start and end apart: 3, of which 3 were waited for; matrix products, arithmetic and copies ran while one was open for 2% of the time, Pallas kernels for 0%

profile of v1, /device:TPU:92, one launch (start us, length us, event | category | flops | bytes accessed | tf_op | source)
XLA Modules:
  0.0 296.7 jit_solution(10076941851399417722)
XLA Ops:
  6.5 0.0 all-gather.2.cloned.1.call-start
  6.5 0.7 all-gather.2.cloned.1.call-update
  7.3 2.2 copy.45
  9.5 6.3 %all_to_all.35 = bf16[16,2,8,24,256]{4,3,2,0,1:T(8,128)(2,1)S(1)} all-to-all(bf16[16,2,8,24,256]{4,3,2,0,1:T(8,128)(2,1)S(1)} %copy.45), channel_id=1, replica_groups=mesh['z'=16,'core'=2,'orb'=16] {'core'}, dimensions={1} | all-to-all | bytes 6291456 | tf_op jit(solution)/shard_map/all_to_all | solution.py:19
  15.7 0.3 copy.46
  16.0 74.2 %all-gather.2.cloned.1.call-done = bf16[16,8,256,64]{2,3,1,0:T(8,128)(2,1)} async-done(((bf16[1,8,256,64]{2,3,1,0:T(8,128)(2,1)}), bf16[16,8,256,64]{2,3,1,0:T(8,128)(2,1)}) %all-gather.2.cloned.1.call-update) | async-done | bytes 4194320 | tf_op jit(solution)/shard_map/all_gather | solution.py:21
  90.2 4.6 %fusion.25 = bf16[16,8,48,64]{3,2,1,0:T(8,128)(2,1)} fusion(bf16[16,8,256,64]{2,3,1,0:T(8,128)(2,1)} %all-gather.2.cloned.1.call-done, bf16[16,8,48,256]{3,2,1,0:T(8,128)(2,1)S(1)} %bitcast.105), kind=kOutput, calls=%fused_computation.56 | convolution fusion | flops 201719808 | bytes 8126464 | tf_op jit(solution)/shard_map/zkfm,zkma->zkaf/dot_general | solution.py:22
  94.8 0.0 copy-start.2
  94.8 0.0 copy-start.1
  94.8 3.9 %reshape.179 = bf16[16,2,12288]{2,1,0:T(2,128)(2,1)} reshape(bf16[16,8,48,64]{3,2,1,0:T(8,128)(2,1)} %fusion.25) | data formatting | bytes 1572864
  98.7 8.3 %all-to-all-start.1 = ((bf16[16,2,12288]{2,1,0:T(2,128)(2,1)}), bf16[16,2,12288]{2,1,0:T(2,128)(2,1)S(1)}, u32[]{:S(2)}, u32[]{:S(2)}) async-start(bf16[16,2,12288]{2,1,0:T(2,128)(2,1)} %reshape.179), calls=%async_computation.1 | async-start | bytes 1572864 | tf_op jit(solution)/shard_map/all_to_all | solution.py:25
  107.0 0.0 copy-done.2
  107.0 0.1 copy.48
  107.0 0.1 fusion.13
  107.1 0.0 copy-done.1
  107.1 0.4 select_reduce_fusion
  107.6 0.1 convert_reduce_fusion
  107.8 0.1 copy.44
  107.9 28.0 %all-to-all-done.1 = bf16[16,2,12288]{2,1,0:T(2,128)(2,1)S(1)} async-done(((bf16[16,2,12288]{2,1,0:T(2,128)(2,1)}), bf16[16,2,12288]{2,1,0:T(2,128)(2,1)S(1)}, u32[]{:S(2)}, u32[]{:S(2)}) %all-to-all-start.1) | async-done | bytes 786464 | tf_op jit(solution)/shard_map/all_to_all | solution.py:25
  135.9 1.0 reshape.180
  136.9 0.1 bitcast_bitcast_fusion
  137.1 3.1 %copy.47 = bf16[1,8,64,16,48]{4,3,2,1,0:T(8,128)(2,1)} copy(bf16[1,8,64,16,48]{2,4,1,3,0:T(8,128)(2,1)S(1)} %bitcast_bitcast_fusion) | data formatting | bytes 1572864 | tf_op jit(solution)/shard_map/all_to_all | solution.py:25
  140.2 5.7 %reshape_squeeze.10 = bf16[8,49152]{1,0:T(8,128)(2,1)S(1)} reshape(bf16[1,8,64,16,48]{4,3,2,1,0:T(8,128)(2,1)} %copy.47) | data formatting | bytes 1572864 | tf_op jit(solution)/shard_map/reshape;squeeze | solution.py:46
  145.9 0.1 constant_dynamic-update-slice_fusion
  146.0 0.1 dynamic-update-slice.1
  146.1 0.2 dynamic-update-slice.2
  146.4 0.2 dynamic-update-slice.3
  146.6 1.6 convolution_convert_fusion
  148.3 5.1 %copy.49 = bf16[16,3,49280]{2,1,0:T(4,128)(2,1)} copy(bf16[16,3,49280]{2,0,1:T(8,128)(2,1)S(1)} %convolution_convert_fusion) | data formatting | bytes 9461760 | tf_op jit(solution)/shard_map/convert_element_type | solution.py:47
  153.3 6.9 %all-to-all-start.2 = ((bf16[16,3,49280]{2,1,0:T(4,128)(2,1)}), bf16[16,3,49280]{2,1,0:T(4,128)(2,1)}, u32[]{:S(2)}, u32[]{:S(2)}) async-start(bf16[16,3,49280]{2,1,0:T(4,128)(2,1)} %copy.49), calls=%async_computation.2 | async-start | bytes 12615680 | tf_op jit(solution)/shard_map/all_to_all | solution.py:50
  160.3 1.2 copy.51
  161.6 82.8 %all-to-all-done.2 = bf16[16,3,49280]{2,1,0:T(4,128)(2,1)} async-done(((bf16[16,3,49280]{2,1,0:T(4,128)(2,1)}), bf16[16,3,49280]{2,1,0:T(4,128)(2,1)}, u32[]{:S(2)}, u32[]{:S(2)}) %all-to-all-start.2) | async-done | bytes 4730912 | tf_op jit(solution)/shard_map/all_to_all | solution.py:50
  244.4 7.3 %reshape.170 = bf16[48,49280]{1,0:T(8,128)(2,1)} reshape(bf16[16,3,49280]{2,1,0:T(4,128)(2,1)} %all-to-all-done.2) | data formatting | bytes 9461760 | tf_op jit(solution)/shard_map/reshape | solution.py:51
  251.6 3.2 %fusion.14 = f32[24,49280]{1,0:T(8,128)S(1)} fusion(bf16[48,49280]{1,0:T(8,128)(2,1)} %reshape.170, s32[24]{0:T(128)S(1)} %add_bitcast_fusion), kind=kOutput, calls=%fused_computation.30 | convolution fusion | flops 113542272 | bytes 9461856 | tf_op jit(solution)/shard_map/ns,sv->nv/dot_general | solution.py:56
  254.8 0.1 fusion.12
  254.9 1.6 slice.26
  256.6 4.7 %reshape.174 = bf16[24,64,6,128,1]{3,2,1,0,4:T(8,128)(2,1)S(1)} reshape(bf16[24,49152]{1,0:T(8,128)(2,1)} %slice.26) | data formatting | bytes 4718592 | tf_op jit(solution)/shard_map/reshape | solution.py:59
  261.3 0.0 copy-start
  261.3 9.1 %convert_bitcast_fusion = bf16[8,24,64,6,128]{4,0,3,2,1:T(8,128)(2,1)} fusion(bf16[24,64,6,128,1]{3,2,1,0,4:T(8,128)(2,1)S(1)} %reshape.174, s32[24,6]{1,0:T(8,128)S(1)} %fusion.12, s32[8,6]{0,1:T(8,128)S(1)} %bitcast.109), kind=kOutput, calls=%fused_computation.3 | convolution fusion | flops 122690304 | bytes 21234432 | tf_op jit(solution)/shard_map/rnbe,nxep->rnxbp/dot_general | solution.py:62
  270.4 0.0 copy-done
  270.4 12.5 %fusion.2 = bf16[8,24,64,64]{2,3,1,0:T(8,128)(2,1)} fusion(bf16[8,64,6,128,1]{1,3,2,4,0:T(8,128)(2,1)S(1)} %bitcast.108, bf16[8,24,64,6,128]{4,0,3,2,1:T(8,128)(2,1)} %convert_bitcast_fusion), kind=kOutput, calls=%fused_computation.6 | convolution fusion | flops 1208745984 | bytes 21233664 | tf_op jit(solution)/shard_map/rabp,rnxbp->rnax/dot_general | solution.py:65
  283.0 3.4 %copy.54 = bf16[8,24,64,64]{3,2,1,0:T(8,128)(2,1)S(1)} copy(bf16[8,24,64,64]{2,3,1,0:T(8,128)(2,1)} %fusion.2) | data formatting | bytes 3145728 | tf_op jit(solution)/shard_map/convert_element_type | solution.py:70
  286.4 3.4 %reshape.172 = bf16[1,8,24,4096]{3,2,1,0:T(8,128)(2,1)} reshape(bf16[8,24,64,64]{3,2,1,0:T(8,128)(2,1)S(1)} %copy.54) | data formatting | bytes 3145728 | tf_op jit(solution)/shard_map/reshape | solution.py:71
  (9 shorter events, 0.1 us)
Async XLA Ops:
  6.5 83.7 %all-gather.2.cloned.1.call-start = ((), (), s32[]{:S(2)}) async-start(), calls=%async_computation.3 | async-start | bytes 4456448 | tf_op jit(solution)/shard_map/all_gather | solution.py:21
  94.8 12.2 %copy-start.2 = (s32[1,8,6]{1,0,2:T(1,128)S(1)}, s32[1,8,6]{1,0,2:T(1,128)}, u32[]{:S(2)}) copy-start(s32[1,8,6]{1,0,2:T(1,128)} %param.6) | copy-start | bytes 580
  94.8 12.3 %copy-start.1 = (s32[1,16,24]{2,1,0:T(8,128)S(1)}, s32[1,16,24]{2,1,0:T(8,128)}, u32[]{:S(2)}) copy-start(s32[1,16,24]{2,1,0:T(8,128)} %param.7) | copy-start | bytes 4612
  98.7 37.3 %all-to-all-start.1 = ((bf16[16,2,12288]{2,1,0:T(2,128)(2,1)}), bf16[16,2,12288]{2,1,0:T(2,128)(2,1)S(1)}, u32[]{:S(2)}, u32[]{:S(2)}) async-start(bf16[16,2,12288]{2,1,0:T(2,128)(2,1)} %reshape.179), calls=%async_computation.1 | async-start | bytes 1572864 | tf_op jit(solution)/shard_map/all_to_all | solution.py:25
  153.3 91.0 %all-to-all-start.2 = ((bf16[16,3,49280]{2,1,0:T(4,128)(2,1)}), bf16[16,3,49280]{2,1,0:T(4,128)(2,1)}, u32[]{:S(2)}, u32[]{:S(2)}) async-start(bf16[16,3,49280]{2,1,0:T(4,128)(2,1)} %copy.49), calls=%async_computation.2 | async-start | bytes 12615680 | tf_op jit(solution)/shard_map/all_to_all | solution.py:50
  261.3 9.2 %copy-start = (bf16[1,8,64,16,48]{2,4,3,1,0:T(8,128)(2,1)S(1)}, bf16[1,8,64,16,48]{2,4,3,1,0:T(8,128)(2,1)}, u32[]{:S(2)}) copy-start(bf16[1,8,64,16,48]{2,4,3,1,0:T(8,128)(2,1)} %copy.51) | copy-start | bytes 2359300
Sparse Core Ops, SparseCore 0:
  9.4 80.7 all-gather.1

commit v2 on v1

--- a/solution.py
+++ b/solution.py
@@ -8,21 +8,31 @@
 FBLK = 6
 CAP = 3
 ORB_DEV = 8
+KA = 4
 
 
-def per_device(half_ints, osv_coef, fit_blocks, partner_list):
+def body(half_ints, osv_coef, fit_blocks, partner_list):
     nz = lax.axis_size("z")
     ncore = lax.axis_size("core")
     rows = half_ints[0]
     n_orb, fchunk, aod = rows.shape
-    rows = rows.reshape(nz, ncore, n_orb // (nz * ncore), fchunk, aod)
-    mine = lax.all_to_all(rows, "core", split_axis=1, concat_axis=3, tiled=True)
-    mine = mine.reshape(nz, n_orb // (nz * ncore), ncore * fchunk, aod)
-    coef = lax.all_gather(osv_coef[0], "z", axis=0, tiled=False)
+    ncol = nz * ncore
+    n_loc = n_orb // ncol
+    rows = rows.reshape(ncol, n_loc, fchunk, aod)
+    coef_own = osv_coef[0]
+    rows_a = lax.all_to_all(rows[:, :KA], ("z", "core"), split_axis=0, concat_axis=2, tiled=True)
+    proj_a = jnp.einsum(
+        "kfm,kma->kaf", rows_a[0], coef_own[:KA], preferred_element_type=jnp.float32
+    ).astype(jnp.bfloat16)
+    rows_b = rows[:, KA:].reshape(nz, ncore, n_loc - KA, fchunk, aod)
+    mine = lax.all_to_all(rows_b, "core", split_axis=1, concat_axis=3, tiled=True)
+    mine = mine.reshape(nz, n_loc - KA, ncore * fchunk, aod)
+    coef = lax.all_gather(coef_own[KA:], "z", axis=0, tiled=False)
     part = jnp.einsum(
         "zkfm,zkma->zkaf", mine, coef, preferred_element_type=jnp.float32
     ).astype(jnp.bfloat16)
-    projected = lax.all_to_all(part, "z", split_axis=0, concat_axis=3, tiled=True)[0]
+    proj_b = lax.all_to_all(part, "z", split_axis=0, concat_axis=3, tiled=True)[0]
+    projected = jnp.concatenate([proj_a, proj_b], axis=0)
     n_loc, nosv, fd = projected.shape
 
     own_blocks = fit_blocks[0]
@@ -78,7 +88,7 @@
     mesh3 = Mesh(devs, ("z", "core", "orb"))
     fit = ("z", "core")
     return jax.shard_map(
-        per_device,
+        body,
         mesh=mesh3,
         in_specs=(
             P("orb", None, fit, None),

time: 297 us -> 375 us (1.26)
  the two profiles are of different devices: /device:TPU:92 before, /device:TPU:85 now
where the time goes in v2:
time: 375 us; the launch traced here: 374 us
  waiting for transfers between devices  240 us (64%)
  local copies, waits for them, and re-layouts  37.3 us (10%)
  matrix products  29.3 us (8%)
  blocking collectives  27.1 us (7%)
  starting transfers between devices  25.9 us (7%)
  between operations  13.6 us (4%)
    all_to_all x1, waiting for transfers between devices, body(): recv = lax.all_to_all(send, 'orb', split_axis=0, concat_axis=0, tiled=True)  110 us
    all_to_all x1, waiting for transfers between devices, body(): lax.all_to_all(rows[:, :KA], ('z', 'core'), split_axis=0, concat_axis=2,...  71 us
    all_gather x1, waiting for transfers between devices, body(): coef = lax.all_gather(coef_own[KA:], 'z', axis=0, tiled=False)  58.8 us
    all_to_all x1, blocking collectives, body(): lax.all_to_all(part, 'z', split_axis=0, concat_axis=3, tiled=True)[0]  21.8 us
    all_to_all x1, starting transfers between devices, body(): lax.all_to_all(rows[:, :KA], ('z', 'core'), split_axis=0, concat_axis=2,...  19.2 us
    dot_general x1, matrix products, body(): jnp.einsum('rabp,rnxbp->rnax', projected.reshape(n_loc, nosv, FBLK, BLK),...  12.5 us
    dot_general x1, matrix products, body(): jnp.einsum('rnbe,nxep->rnxbp', match, prow, preferred_element_type=jnp.fl...  9.15 us
  transfers between devices with their start and end apart: 3, of which 3 were waited for; matrix products, arithmetic and copies ran while one was open for 2% of the time, Pallas kernels for 0%

profile of v2, /device:TPU:85, one launch (start us, length us, event | category | flops | bytes accessed | tf_op | source)
XLA Modules:
  0.0 374.2 jit_solution(5032144984455290349)
XLA Ops:
  6.5 1.6 slice.32
  8.1 0.0 all-gather.2.cloned.1.call-update
  8.1 3.2 fusion.30
  11.4 0.1 copy.44
  11.5 5.3 %all_to_all.50 = bf16[16,2,4,24,256]{4,3,2,0,1:T(8,128)(2,1)S(1)} all-to-all(bf16[16,2,4,24,256]{4,3,2,0,1:T(8,128)(2,1)S(1)} %copy.44), channel_id=1, replica_groups=mesh['z'=16,'core'=2,'orb'=16] {'core'}, dimensions={1} | all-to-all | bytes 3145728 | tf_op jit(solution)/shard_map/all_to_all | solution.py:28
  16.8 0.1 copy.45
  16.9 58.8 %all-gather.2.cloned.1.call-done = bf16[16,4,256,64]{2,3,1,0:T(8,128)(2,1)} async-done(((bf16[1,4,256,64]{2,3,1,0:T(8,128)(2,1)}), bf16[16,4,256,64]{2,3,1,0:T(8,128)(2,1)}) %all-gather.2.cloned.1.call-update) | async-done | bytes 2097168 | tf_op jit(solution)/shard_map/all_gather | solution.py:30
  75.7 2.3 fusion.31
  78.0 0.0 copy-start.4
  78.0 0.0 copy-start.3
  78.0 0.5 reshape.194
  78.5 21.8 %all_to_all.51 = bf16[16,2,6144]{2,1,0:T(2,128)(2,1)S(1)} all-to-all(bf16[16,2,6144]{2,1,0:T(2,128)(2,1)S(1)} %reshape.194), channel_id=1, replica_groups=mesh['z'=16,'core'=2,'orb'=16] {'z'}, dimensions={0} | all-to-all | bytes 786432 | tf_op jit(solution)/shard_map/all_to_all | solution.py:34
  100.3 19.2 %all-to-all-start = ((bf16[32,4,24,256]{3,2,1,0:T(8,128)(2,1)}), bf16[32,4,24,256]{3,2,1,0:T(8,128)(2,1)S(1)}, u32[]{:S(2)}, u32[]{:S(2)}) async-start(bf16[32,4,24,256]{3,2,1,0:T(8,128)(2,1)} %get-tuple-element.7), calls=%async_computation | async-start | bytes 3145728 | tf_op jit(solution)/shard_map/all_to_all | solution.py:23
  119.6 0.0 copy-done.4
  119.6 0.1 copy.47
  119.7 0.1 fusion.17
  119.7 0.4 select_reduce_fusion
  120.3 0.1 convert_reduce_fusion
  120.4 0.1 copy.42
  120.5 0.5 reshape.195
  121.0 0.1 bitcast_bitcast_fusion
  121.1 1.0 copy.46
  122.1 2.2 concatenate.22
  124.3 71.0 %all-to-all-done = bf16[32,4,24,256]{3,2,1,0:T(8,128)(2,1)S(1)} async-done(((bf16[32,4,24,256]{3,2,1,0:T(8,128)(2,1)}), bf16[32,4,24,256]{3,2,1,0:T(8,128)(2,1)S(1)}, u32[]{:S(2)}, u32[]{:S(2)}) %all-to-all-start) | async-done | bytes 1572896 | tf_op jit(solution)/shard_map/all_to_all | solution.py:23
  195.3 0.1 copy.43
  195.4 0.6 convolution_convert_fusion.2
  196.0 0.3 copy.61
  196.3 0.4 maximum_dynamic-update-slice_fusion
  196.7 0.1 dynamic-update-slice.1
  196.9 0.2 dynamic-update-slice.2
  197.1 0.2 dynamic-update-slice.3
  197.4 1.7 convolution_convert_fusion
  199.1 5.1 %copy.48 = bf16[16,3,49280]{2,1,0:T(4,128)(2,1)} copy(bf16[16,3,49280]{2,0,1:T(8,128)(2,1)S(1)} %convolution_convert_fusion) | data formatting | bytes 9461760 | tf_op jit(solution)/shard_map/convert_element_type | solution.py:57
  204.1 6.7 %all-to-all-start.3 = ((bf16[16,3,49280]{2,1,0:T(4,128)(2,1)}), bf16[16,3,49280]{2,1,0:T(4,128)(2,1)}, u32[]{:S(2)}, u32[]{:S(2)}) async-start(bf16[16,3,49280]{2,1,0:T(4,128)(2,1)} %copy.48), calls=%async_computation.3 | async-start | bytes 12615680 | tf_op jit(solution)/shard_map/all_to_all | solution.py:60
  210.8 0.1 copy.50
  210.9 1.0 copy.52
  211.9 0.1 copy_bitcast_fusion
  212.0 109.9 %all-to-all-done.3 = bf16[16,3,49280]{2,1,0:T(4,128)(2,1)} async-done(((bf16[16,3,49280]{2,1,0:T(4,128)(2,1)}), bf16[16,3,49280]{2,1,0:T(4,128)(2,1)}, u32[]{:S(2)}, u32[]{:S(2)}) %all-to-all-start.3) | async-done | bytes 4730912 | tf_op jit(solution)/shard_map/all_to_all | solution.py:60
  321.9 7.3 %reshape.185 = bf16[48,49280]{1,0:T(8,128)(2,1)} reshape(bf16[16,3,49280]{2,1,0:T(4,128)(2,1)} %all-to-all-done.3) | data formatting | bytes 9461760 | tf_op jit(solution)/shard_map/reshape | solution.py:61
  329.2 3.2 fusion.18
  332.4 0.1 fusion.16
  332.5 1.7 slice.53
  334.1 4.7 %reshape.189 = bf16[24,64,6,128,1]{3,2,1,0,4:T(8,128)(2,1)S(1)} reshape(bf16[24,49152]{1,0:T(8,128)(2,1)} %slice.53) | data formatting | bytes 4718592 | tf_op jit(solution)/shard_map/reshape | solution.py:69
  338.9 0.0 copy-start.1
  338.9 9.1 %convert_bitcast_fusion = bf16[8,24,64,6,128]{4,0,3,2,1:T(8,128)(2,1)} fusion(bf16[24,64,6,128,1]{3,2,1,0,4:T(8,128)(2,1)S(1)} %reshape.189, s32[24,6]{1,0:T(8,128)S(1)} %fusion.16, s32[8,6]{0,1:T(8,128)S(1)} %bitcast.130), kind=kOutput, calls=%fused_computation.3 | convolution fusion | flops 122690304 | bytes 21234432 | tf_op jit(solution)/shard_map/rnbe,nxep->rnxbp/dot_general | solution.py:72
  348.0 12.5 %fusion.2 = bf16[8,24,64,64]{2,3,1,0:T(8,128)(2,1)} fusion(bf16[8,24,64,6,128]{4,0,3,2,1:T(8,128)(2,1)} %convert_bitcast_fusion, bf16[4,64,6,128]{3,1,2,0:T(8,128)(2,1)S(1)} %copy-done.1, bf16[4,64,6,128]{3,1,2,0:T(8,128)(2,1)S(1)} %copy_bitcast_fusion), kind=kOutput, calls=%fused_computation.6 | convolution fusion | flops 1209139200 | bytes 21233664 | tf_op jit(solution)/shard_map/rabp,rnxbp->rnax/dot_general | solution.py:75
  360.5 3.4 copy.54
  364.0 3.4 reshape.187
  (16 shorter events, 0.1 us)
Async XLA Ops:
  6.5 69.1 %all-gather.2.cloned.1.call-start = ((), (), s32[]{:S(2)}) async-start(), calls=%async_computation.4 | async-start | bytes 2228224 | tf_op jit(solution)/shard_map/all_gather | solution.py:30
  78.0 41.6 %copy-start.4 = (s32[1,8,6]{1,0,2:T(1,128)S(1)}, s32[1,8,6]{1,0,2:T(1,128)}, u32[]{:S(2)}) copy-start(s32[1,8,6]{1,0,2:T(1,128)} %param.6) | copy-start | bytes 580
  78.0 41.8 %copy-start.3 = (s32[1,16,24]{2,1,0:T(8,128)S(1)}, s32[1,16,24]{2,1,0:T(8,128)}, u32[]{:S(2)}) copy-start(s32[1,16,24]{2,1,0:T(8,128)} %param.7) | copy-start | bytes 4612
  100.3 95.0 %all-to-all-start = ((bf16[32,4,24,256]{3,2,1,0:T(8,128)(2,1)}), bf16[32,4,24,256]{3,2,1,0:T(8,128)(2,1)S(1)}, u32[]{:S(2)}, u32[]{:S(2)}) async-start(bf16[32,4,24,256]{3,2,1,0:T(8,128)(2,1)} %get-tuple-element.7), calls=%async_computation | async-start | bytes 3145728 | tf_op jit(solution)/shard_map/all_to_all | solution.py:23
  124.3 71.2 %copy-start.2 = (bf16[1,8,256,64]{2,3,1,0:T(8,128)(2,1)S(1)}, bf16[1,8,256,64]{2,3,1,0:T(8,128)(2,1)}, u32[]{:S(2)}) copy-start(bf16[1,8,256,64]{2,3,1,0:T(8,128)(2,1)} %param.5) | copy-start | bytes 786436
  124.3 72.1 %copy-start = (bf16[4,49152]{1,0:T(4,128)(2,1)S(1)}, bf16[4,49152]{1,0:T(4,128)(2,1)}, u32[]{:S(2)}) copy-start(bf16[4,49152]{1,0:T(4,128)(2,1)} %concatenate.22) | copy-start | bytes 1179652
  204.1 117.8 %all-to-all-start.3 = ((bf16[16,3,49280]{2,1,0:T(4,128)(2,1)}), bf16[16,3,49280]{2,1,0:T(4,128)(2,1)}, u32[]{:S(2)}, u32[]{:S(2)}) async-start(bf16[16,3,49280]{2,1,0:T(4,128)(2,1)} %copy.48), calls=%async_computation.3 | async-start | bytes 12615680 | tf_op jit(solution)/shard_map/all_to_all | solution.py:60
  338.9 9.2 %copy-start.1 = (bf16[4,64,6,128]{3,1,2,0:T(8,128)(2,1)S(1)}, bf16[4,64,6,128]{3,1,2,0:T(8,128)(2,1)}, u32[]{:S(2)}) copy-start(bf16[4,64,6,128]{3,1,2,0:T(8,128)(2,1)} %copy.52) | copy-start | bytes 1179652
Sparse Core Ops, SparseCore 0:
  9.4 66.2 all-gather.1

commit v3 on v1

--- a/solution.py
+++ b/solution.py
@@ -1,7 +1,10 @@
+import functools
 import jax
 import jax.numpy as jnp
 import numpy as np
 from jax import lax
+from jax.experimental import pallas as pl
+from jax.experimental.pallas import tpu as pltpu
 from jax.sharding import Mesh, PartitionSpec as P
 
 BLK = 128
@@ -40,35 +43,75 @@
         & (sub[:, :, None, None] == jnp.arange(n_loc)[None, None, None, :])
     )
     sel = jnp.sum(sel.astype(jnp.float32), axis=1).astype(jnp.bfloat16)
+    nblk = fd // BLK
+    code_rows = 8
     code = jnp.concatenate(
-        [own_blocks // 8, own_blocks % 8, jnp.zeros((n_loc, 128 - 2 * FBLK), jnp.int32)], axis=1
+        [own_blocks // 8, own_blocks % 8, jnp.zeros((n_loc, BLK - 2 * FBLK), jnp.int32)], axis=1
     ).astype(jnp.bfloat16)
-    payload = jnp.concatenate([projected.reshape(n_loc, nosv * fd), code], axis=1)
-    send = jnp.einsum("dsk,kv->dsv", sel, payload, preferred_element_type=jnp.float32).astype(
+    code = jnp.concatenate(
+        [code[:, None, :], jnp.zeros((n_loc, code_rows - 1, BLK), jnp.bfloat16)], axis=1
+    )
+    blocks_major = projected.reshape(n_loc, nosv, nblk, BLK).transpose(0, 2, 1, 3)
+    payload = jnp.concatenate([blocks_major.reshape(n_loc, nblk * nosv, BLK), code], axis=1)
+    send = jnp.einsum("dsk,kyp->dsyp", sel, payload, preferred_element_type=jnp.float32).astype(
         jnp.bfloat16
     )
     recv = lax.all_to_all(send, "orb", split_axis=0, concat_axis=0, tiled=True)
-    recv = recv.reshape(ngroups * CAP, -1)
+    recv = recv.reshape(ngroups * CAP, nblk * nosv + code_rows, BLK)
     my_owner = lax.dynamic_index_in_dim(owner, me, 0, keepdims=False)
     my_rank = lax.dynamic_index_in_dim(rank, me, 0, keepdims=False)
-    slot = my_owner * CAP + my_rank
-    pick = (slot[:, None] == jnp.arange(ngroups * CAP)[None, :]).astype(jnp.bfloat16)
-    partner = jnp.einsum("ns,sv->nv", pick, recv, preferred_element_type=jnp.float32)
-    pcode = partner[:, nosv * fd : nosv * fd + 2 * FBLK]
+    slot = (my_owner * CAP + my_rank).astype(jnp.int32)
+    pick = (slot[:, None] == jnp.arange(ngroups * CAP)[None, :]).astype(jnp.float32)
+    codes = recv[:, nblk * nosv, : 2 * FBLK].astype(jnp.float32)
+    pcode = jnp.einsum("ns,sc->nc", pick, codes)
     pblocks = (pcode[:, :FBLK] * 8 + pcode[:, FBLK:]).astype(jnp.int32)
-    prow = partner[:, : nosv * fd].astype(jnp.bfloat16).reshape(npart, nosv, FBLK, BLK)
+    match = own_blocks[:, None, :, None] == pblocks[None, :, None, :]
+    eidx = jnp.sum(jnp.where(match, jnp.arange(1, FBLK + 1)[None, None, None, :], 0), axis=3) - 1
+    res = pair_call(slot, eidx.astype(jnp.int32).reshape(-1), projected, recv)
+    pair = res.reshape(n_loc, nosv, npart, nosv).transpose(0, 2, 1, 3)
+    return pair.reshape(1, n_loc, npart, nosv * nosv)
 
-    match = (own_blocks[:, None, :, None] == pblocks[None, :, None, :]).astype(jnp.bfloat16)
-    aligned = jnp.einsum(
-        "rnbe,nxep->rnxbp", match, prow, preferred_element_type=jnp.float32
-    ).astype(jnp.bfloat16)
-    pair = jnp.einsum(
-        "rabp,rnxbp->rnax",
-        projected.reshape(n_loc, nosv, FBLK, BLK),
-        aligned,
-        preferred_element_type=jnp.float32,
-    ).astype(jnp.bfloat16)
-    return pair.reshape(1, n_loc, npart, nosv * nosv)
+
+def pair_kernel(slot_ref, eidx_ref, own_ref, recv_ref, out_ref, a_ref, *, npart, nosv):
+    r = pl.program_id(0)
+
+    def fill(n, carry):
+        s = slot_ref[n]
+        for b in range(FBLK):
+            e = eidx_ref[(r * npart + n) * FBLK + b]
+            ee = jnp.maximum(e, 0)
+            blk = recv_ref[s, pl.ds(pl.multiple_of(ee * nosv, nosv), nosv), :]
+            blk = jnp.where(e >= 0, blk, jnp.zeros_like(blk))
+            a_ref[pl.ds(pl.multiple_of(n * nosv, nosv), nosv), pl.ds(b * BLK, BLK)] = blk
+        return carry
+
+    lax.fori_loop(0, npart, fill, 0)
+    res = lax.dot_general(
+        own_ref[0], a_ref[...], (((1,), (1,)), ((), ())), preferred_element_type=jnp.float32
+    )
+    out_ref[0] = res.astype(out_ref.dtype)
+
+
+def pair_call(slot, eidx, own, recv, interpret=False):
+    n_loc, nosv, fd = own.shape
+    npart = slot.shape[0]
+    nslot, rows, _ = recv.shape
+    kern = functools.partial(pair_kernel, npart=npart, nosv=nosv)
+    return pl.pallas_call(
+        kern,
+        out_shape=jax.ShapeDtypeStruct((n_loc, nosv, npart * nosv), jnp.bfloat16),
+        grid_spec=pltpu.PrefetchScalarGridSpec(
+            num_scalar_prefetch=2,
+            grid=(n_loc,),
+            in_specs=[
+                pl.BlockSpec((1, nosv, fd), lambda r, s, e: (r, 0, 0)),
+                pl.BlockSpec((nslot, rows, BLK), lambda r, s, e: (0, 0, 0)),
+            ],
+            out_specs=pl.BlockSpec((1, nosv, npart * nosv), lambda r, s, e: (r, 0, 0)),
+            scratch_shapes=[pltpu.VMEM((npart * nosv, fd), jnp.bfloat16)],
+        ),
+        interpret=interpret,
+    )(slot, eidx, own, recv)
 
 
 def solution(mesh):

time: 297 us -> 256 us (0.86)
  the two profiles are of different devices: /device:TPU:92 before, /device:TPU:116 now
where the time goes in v3:
time: 256 us
  waiting for transfers between devices  156 us (61%)
  local copies, waits for them, and re-layouts  33.8 us (13%)
  Pallas kernels  19 us (7%)
  starting transfers between devices  16 us (6%)
  between operations  13.5 us (5%)
  matrix products  9.6 us (4%)
  blocking collectives  6.26 us (2%)
    all_gather x1, waiting for transfers between devices, per_device(): coef = lax.all_gather(osv_coef[0], 'z', axis=0, tiled=False)  73.4 us
    all_to_all x1, waiting for transfers between devices, per_device(): recv = lax.all_to_all(send, 'orb', split_axis=0, concat_axis=0, tiled=True)  55.3 us
    all_to_all x1, waiting for transfers between devices, per_device(): lax.all_to_all(part, 'z', split_axis=0, concat_axis=3, tiled=True)[0]  27.1 us
    pallas_call x1, Pallas kernels, pair_call(): pl.pallas_call(kern, out_shape=jax.ShapeDtypeStruct((n_loc, nosv, npart *...  19 us
    all_to_all x1, starting transfers between devices, per_device(): lax.all_to_all(part, 'z', split_axis=0, concat_axis=3, tiled=True)[0]  8.78 us
    all_to_all x1, starting transfers between devices, per_device(): recv = lax.all_to_all(send, 'orb', split_axis=0, concat_axis=0, tiled=True)  7.23 us
    all_to_all x1, blocking collectives, per_device(): mine = lax.all_to_all(rows, 'core', split_axis=1, concat_axis=3, tiled=True)  6.26 us
    reshape x1, local copies, waits for them, and re-layouts, per_device(): return pair.reshape(1, n_loc, npart, nosv * nosv)  5.15 us
  transfers between devices with their start and end apart: 3, of which 3 were waited for; matrix products, arithmetic and copies ran while one was open for 4% of the time, Pallas kernels for 0%

profile of v3, /device:TPU:116, one launch (start us, length us, event | category | flops | bytes accessed | tf_op | source)
XLA Modules:
  0.0 255.5 jit_solution(14854738236780104188)
XLA Ops:
  6.5 0.0 all-gather.2.cloned.1.call-start
  6.5 0.7 all-gather.2.cloned.1.call-update
  7.3 2.2 copy.54
  9.5 6.3 %all_to_all.35 = bf16[16,2,8,24,256]{4,3,2,0,1:T(8,128)(2,1)S(1)} all-to-all(bf16[16,2,8,24,256]{4,3,2,0,1:T(8,128)(2,1)S(1)} %copy.54), channel_id=1, replica_groups=mesh['z'=16,'core'=2,'orb'=16] {'core'}, dimensions={1} | all-to-all | bytes 6291456 | tf_op jit(solution)/shard_map/all_to_all | solution.py:22
  15.7 0.3 copy.55
  16.0 73.4 %all-gather.2.cloned.1.call-done = bf16[16,8,256,64]{2,3,1,0:T(8,128)(2,1)} async-done(((bf16[1,8,256,64]{2,3,1,0:T(8,128)(2,1)}), bf16[16,8,256,64]{2,3,1,0:T(8,128)(2,1)}) %all-gather.2.cloned.1.call-update) | async-done | bytes 4194320 | tf_op jit(solution)/shard_map/all_gather | solution.py:24
  89.4 4.6 %fusion.27 = bf16[16,8,48,64]{3,2,1,0:T(8,128)(2,1)} fusion(bf16[16,8,256,64]{2,3,1,0:T(8,128)(2,1)} %all-gather.2.cloned.1.call-done, bf16[16,8,48,256]{3,2,1,0:T(8,128)(2,1)S(1)} %bitcast.102), kind=kOutput, calls=%fused_computation.60 | convolution fusion | flops 201719808 | bytes 8126464 | tf_op jit(solution)/shard_map/zkfm,zkma->zkaf/dot_general | solution.py:25
  93.9 0.0 copy-start.1
  93.9 0.0 copy-start
  93.9 3.9 %reshape.225 = bf16[16,2,12288]{2,1,0:T(2,128)(2,1)} reshape(bf16[16,8,48,64]{3,2,1,0:T(8,128)(2,1)} %fusion.27) | data formatting | bytes 1572864
  97.8 8.8 %all-to-all-start.1 = ((bf16[16,2,12288]{2,1,0:T(2,128)(2,1)}), bf16[16,2,12288]{2,1,0:T(2,128)(2,1)S(1)}, u32[]{:S(2)}, u32[]{:S(2)}) async-start(bf16[16,2,12288]{2,1,0:T(2,128)(2,1)} %reshape.225), calls=%async_computation.1 | async-start | bytes 1572864 | tf_op jit(solution)/shard_map/all_to_all | solution.py:28
  106.6 0.0 copy-done.1
  106.6 0.1 copy.51
  106.7 0.1 fusion.9
  106.8 0.0 copy-done
  106.8 0.4 select_reduce_fusion
  107.3 0.1 convert_reduce_fusion
  107.4 0.1 copy.53
  107.5 0.1 pad.4.clone
  107.6 0.1 pad.3.clone
  107.7 27.1 %all-to-all-done.1 = bf16[16,2,12288]{2,1,0:T(2,128)(2,1)S(1)} async-done(((bf16[16,2,12288]{2,1,0:T(2,128)(2,1)}), bf16[16,2,12288]{2,1,0:T(2,128)(2,1)S(1)}, u32[]{:S(2)}, u32[]{:S(2)}) %all-to-all-start.1) | async-done | bytes 786464 | tf_op jit(solution)/shard_map/all_to_all | solution.py:28
  134.8 1.0 reshape.226
  135.8 0.1 bitcast_bitcast_fusion
  135.9 0.1 copy.56
  136.0 1.5 copy.57
  137.5 4.8 %convolution_convert_fusion = bf16[16,3,392,128]{3,0,2,1:T(8,128)(2,1)S(1)} fusion(bf16[8,1,6]{2,0,1:T(8,128)(2,1)S(1)} %get-tuple-element.8, bf16[8,1,6]{2,0,1:T(8,128)(2,1)S(1)} %get-tuple-element.7, bf16[8,384,128]{2,0,1:T(8,128)(2,1)} %bitcast.107, bf16[392]{0:T(512)(128)(2,1)S(1)} %pad.4.clone, bf16[392,128]{1,0:T(8,128)(2,1)S(1)} %pad.3.clone, ...), kind=kOutput, calls=%fused_computation | convolution fusion | flops 44957696 | bytes 5705424 | tf_op jit(solution)/shard_map/dsk,kyp->dsyp/dot_general | solution.py:56
  142.4 3.4 %copy.58 = bf16[16,3,392,128]{3,2,1,0:T(8,128)(2,1)} copy(bf16[16,3,392,128]{3,0,2,1:T(8,128)(2,1)S(1)} %convolution_convert_fusion) | data formatting | bytes 9633792 | tf_op jit(solution)/shard_map/convert_element_type | solution.py:56
  145.8 7.2 %all-to-all-start.2 = ((bf16[16,3,392,128]{3,2,1,0:T(8,128)(2,1)}), bf16[16,3,392,128]{3,2,1,0:T(8,128)(2,1)}, u32[]{:S(2)}, u32[]{:S(2)}) async-start(bf16[16,3,392,128]{3,2,1,0:T(8,128)(2,1)} %copy.58), calls=%async_computation.2 | async-start | bytes 9633792 | tf_op jit(solution)/shard_map/all_to_all | solution.py:59
  153.1 0.0 copy-start.2
  153.1 3.1 %copy.61 = bf16[1,8,64,16,48]{4,3,2,1,0:T(8,128)(2,1)} copy(bf16[1,8,64,16,48]{2,4,1,3,0:T(8,128)(2,1)S(1)} %bitcast_bitcast_fusion) | data formatting | bytes 1572864 | tf_op jit(solution)/shard_map/all_to_all | solution.py:28
  156.2 4.3 %squeeze.15.own_ref = bf16[8,64,768]{2,1,0:T(8,128)(2,1)} reshape(bf16[1,8,64,16,48]{4,3,2,1,0:T(8,128)(2,1)} %copy.61) | data formatting | bytes 1572864 | tf_op jit(solution)/shard_map/squeeze | solution.py:28
  160.5 55.3 %all-to-all-done.2 = bf16[16,3,392,128]{3,2,1,0:T(8,128)(2,1)} async-done(((bf16[16,3,392,128]{3,2,1,0:T(8,128)(2,1)}), bf16[16,3,392,128]{3,2,1,0:T(8,128)(2,1)}, u32[]{:S(2)}, u32[]{:S(2)}) %all-to-all-start.2) | async-done | bytes 4816928 | tf_op jit(solution)/shard_map/all_to_all | solution.py:59
  215.9 0.9 slice.12
  216.8 0.1 copy.59
  216.9 0.0 copy-done.2
  216.9 0.2 fusion.10
  217.1 0.1 select_reduce_fusion.1
  217.2 0.1 copy.60
  217.3 0.7 sub.21.eidx_ref
  218.1 19.0 %shard_map.46 = bf16[8,64,1536]{2,1,0:T(8,128)(2,1)} custom-call(s32[24]{0:T(128)} %copy-done.2, s32[1152]{0:T(1024)} %sub.21.eidx_ref, bf16[8,64,768]{2,1,0:T(8,128)(2,1)} %squeeze.15.own_ref, bf16[48,392,128]{2,1,0:T(8,128)(2,1)} %bitcast.18.recv_ref), custom_call_target="tpu_custom_call" | custom-call | tf_op jit(solution)/shard_map/pallas_call | solution.py:100
  237.0 4.0 %reshape.221 = bf16[8,64,24,64]{3,2,1,0:T(8,128)(2,1)S(1)} reshape(bf16[8,64,1536]{2,1,0:T(8,128)(2,1)} %shard_map.46) | data formatting | bytes 3145728 | tf_op jit(solution)/shard_map/reshape | solution.py:71
  241.0 2.5 copy.62
  243.5 5.2 %reshape.222 = bf16[1,8,24,4096]{3,2,1,0:T(8,128)(2,1)} reshape(bf16[8,24,64,64]{3,2,1,0:T(8,128)(2,1)} %copy.62) | data formatting | bytes 3145728 | tf_op jit(solution)/shard_map/reshape | solution.py:72
  (13 shorter events, 0.1 us)
Async XLA Ops:
  6.5 82.9 %all-gather.2.cloned.1.call-start = ((), (), s32[]{:S(2)}) async-start(), calls=%async_computation.3 | async-start | bytes 4456448 | tf_op jit(solution)/shard_map/all_gather | solution.py:24
  93.9 12.6 %copy-start.1 = (s32[1,8,6]{1,0,2:T(1,128)S(1)}, s32[1,8,6]{1,0,2:T(1,128)}, u32[]{:S(2)}) copy-start(s32[1,8,6]{1,0,2:T(1,128)} %param.6) | copy-start | bytes 580
  93.9 12.8 %copy-start = (s32[1,16,24]{2,1,0:T(8,128)S(1)}, s32[1,16,24]{2,1,0:T(8,128)}, u32[]{:S(2)}) copy-start(s32[1,16,24]{2,1,0:T(8,128)} %param.7) | copy-start | bytes 4612
  97.8 37.0 %all-to-all-start.1 = ((bf16[16,2,12288]{2,1,0:T(2,128)(2,1)}), bf16[16,2,12288]{2,1,0:T(2,128)(2,1)S(1)}, u32[]{:S(2)}, u32[]{:S(2)}) async-start(bf16[16,2,12288]{2,1,0:T(2,128)(2,1)} %reshape.225), calls=%async_computation.1 | async-start | bytes 1572864 | tf_op jit(solution)/shard_map/all_to_all | solution.py:28
  145.8 70.0 %all-to-all-start.2 = ((bf16[16,3,392,128]{3,2,1,0:T(8,128)(2,1)}), bf16[16,3,392,128]{3,2,1,0:T(8,128)(2,1)}, u32[]{:S(2)}, u32[]{:S(2)}) async-start(bf16[16,3,392,128]{3,2,1,0:T(8,128)(2,1)} %copy.58), calls=%async_computation.2 | async-start | bytes 9633792 | tf_op jit(solution)/shard_map/all_to_all | solution.py:59
  153.1 63.8 %copy-start.2 = (s32[24]{0:T(128)}, s32[24]{0:T(128)S(1)}, u32[]{:S(2)}) copy-start(s32[24]{0:T(128)S(1)} %add_bitcast_fusion.slot_ref) | copy-start | bytes 292
Sparse Core Ops, SparseCore 0:
  9.4 79.9 all-gather.1

commit v4 on v3

--- a/solution.py
+++ b/solution.py
@@ -21,10 +21,31 @@
     rows = rows.reshape(nz, ncore, n_orb // (nz * ncore), fchunk, aod)
     mine = lax.all_to_all(rows, "core", split_axis=1, concat_axis=3, tiled=True)
     mine = mine.reshape(nz, n_orb // (nz * ncore), ncore * fchunk, aod)
-    coef = lax.all_gather(osv_coef[0], "z", axis=0, tiled=False)
-    part = jnp.einsum(
-        "zkfm,zkma->zkaf", mine, coef, preferred_element_type=jnp.float32
-    ).astype(jnp.bfloat16)
+    coef0 = osv_coef[0]
+    zi = lax.axis_index("z")
+    right = [(i, (i + 1) % nz) for i in range(nz)]
+    left = [(i, (i - 1) % nz) for i in range(nz)]
+    chunks = [None] * nz
+    chunks[0] = coef0
+    go_r = coef0
+    go_l = coef0
+    for t in range(1, nz // 2 + 1):
+        go_r = lax.ppermute(go_r, "z", right)
+        chunks[(nz - t) % nz] = go_r
+        if t < nz - t:
+            go_l = lax.ppermute(go_l, "z", left)
+            chunks[t] = go_l
+    parts = []
+    for d in range(nz):
+        rows_d = lax.dynamic_index_in_dim(mine, (zi + d) % nz, 0, keepdims=False)
+        parts.append(
+            jnp.einsum(
+                "kfm,kma->kaf", rows_d, chunks[d], preferred_element_type=jnp.float32
+            ).astype(jnp.bfloat16)
+        )
+    part_rel = jnp.stack(parts)
+    doubled = jnp.concatenate([part_rel, part_rel], axis=0)
+    part = lax.dynamic_slice_in_dim(doubled, (nz - zi) % nz, nz, 0)
     projected = lax.all_to_all(part, "z", split_axis=0, concat_axis=3, tiled=True)[0]
     n_loc, nosv, fd = projected.shape
 

time: 256 us -> 291 us (1.14)
  the two profiles are of different devices: /device:TPU:116 before, /device:TPU:316 now
where the time goes in v4:
time: 291 us; the launch traced here: 290 us
  waiting for transfers between devices  123 us (42%)
  starting transfers between devices  72.8 us (25%)
  local copies, waits for them, and re-layouts  46.9 us (16%)
  matrix products  26.8 us (9%)
  Pallas kernels  19 us (7%)
    all_to_all x1, waiting for transfers between devices, per_device(): recv = lax.all_to_all(send, 'orb', split_axis=0, concat_axis=0, tiled=True)  69.8 us
    all_to_all x1, waiting for transfers between devices, per_device(): lax.all_to_all(part, 'z', split_axis=0, concat_axis=3, tiled=True)[0]  30.8 us
    ppermute x7, starting transfers between devices, per_device(): go_l = lax.ppermute(go_l, 'z', left)  30.4 us
    dot_general x16, matrix products, per_device(): jnp.einsum('kfm,kma->kaf', rows_d, chunks[d], preferred_element_type=jnp....  21.7 us
    pallas_call x1, Pallas kernels, pair_call(): pl.pallas_call(kern, out_shape=jax.ShapeDtypeStruct((n_loc, nosv, npart *...  19 us
    ppermute x8, waiting for transfers between devices, per_device(): go_r = lax.ppermute(go_r, 'z', right)  18.8 us
    ppermute x8, starting transfers between devices, per_device(): go_r = lax.ppermute(go_r, 'z', right)  17.8 us
    unnamed x43, local copies, waits for them, and re-layouts  15.7 us
  transfers between devices with their start and end apart: 18, of which 9 were waited for; matrix products, arithmetic and copies ran while one was open for 9% of the time, Pallas kernels for 0%

profile of v4, /device:TPU:316, one launch (start us, length us, event | category | flops | bytes accessed | tf_op | source)
XLA Modules:
  0.0 289.7 jit_solution(10866498216271079068)
XLA Ops:
  0.0 2.9 %collective-permute-start.7 = (bf16[8,256,64]{1,2,0:T(8,128)(2,1)}, bf16[8,256,64]{1,2,0:T(8,128)(2,1)S(1)}, u32[]{:S(2)}, u32[]{:S(2)}) collective-permute-start(bf16[8,256,64]{1,2,0:T(8,128)(2,1)} %bitcast.285), channel_id=1, source_target_pairs={{0,32},{32,64},{64,96},{96,128},{128,160},{160,192},{192,224},{224... | collective-permute-start | bytes 786440 | tf_op jit(solution)/shard_map/ppermute | solution.py:33
  2.9 2.9 %collective-permute-start = (bf16[8,256,64]{1,2,0:T(8,128)(2,1)}, bf16[8,256,64]{1,2,0:T(8,128)(2,1)S(1)}, u32[]{:S(2)}, u32[]{:S(2)}) collective-permute-start(bf16[8,256,64]{1,2,0:T(8,128)(2,1)} %bitcast.286), channel_id=1, source_target_pairs={{0,480},{32,0},{64,32},{96,64},{128,96},{160,128},{192,160},{224,1... | collective-permute-start | bytes 786440 | tf_op jit(solution)/shard_map/ppermute | solution.py:36
  5.9 4.3 %collective-permute-done.7 = bf16[8,256,64]{1,2,0:T(8,128)(2,1)S(1)} collective-permute-done((bf16[8,256,64]{1,2,0:T(8,128)(2,1)}, bf16[8,256,64]{1,2,0:T(8,128)(2,1)S(1)}, u32[]{:S(2)}, u32[]{:S(2)}) %collective-permute-start.7) | collective-permute-done | bytes 262176 | tf_op jit(solution)/shard_map/ppermute | solution.py:33
  10.8 2.9 %collective-permute-start.8 = (bf16[8,256,64]{1,2,0:T(8,128)(2,1)S(1)}, bf16[8,256,64]{1,2,0:T(8,128)(2,1)S(1)}, u32[]{:S(2)}, u32[]{:S(2)}) collective-permute-start(bf16[8,256,64]{1,2,0:T(8,128)(2,1)S(1)} %collective-permute-done.7), channel_id=1, source_target_pairs={{0,32},{32,64},{64,96},{96,128},{128,160},{160,192},{192,224},{224... | collective-permute-start | bytes 786440 | tf_op jit(solution)/shard_map/ppermute | solution.py:33
  13.8 3.1 %collective-permute-start.1 = (bf16[8,256,64]{1,2,0:T(8,128)(2,1)S(1)}, bf16[8,256,64]{1,2,0:T(8,128)(2,1)S(1)}, u32[]{:S(2)}, u32[]{:S(2)}) collective-permute-start(bf16[8,256,64]{1,2,0:T(8,128)(2,1)S(1)} %collective-permute-done), channel_id=1, source_target_pairs={{0,480},{32,0},{64,32},{96,64},{128,96},{160,128},{192,160},{224,1... | collective-permute-start | bytes 786440 | tf_op jit(solution)/shard_map/ppermute | solution.py:36
  16.9 3.5 %collective-permute-done.8 = bf16[8,256,64]{1,2,0:T(8,128)(2,1)S(1)} collective-permute-done((bf16[8,256,64]{1,2,0:T(8,128)(2,1)S(1)}, bf16[8,256,64]{1,2,0:T(8,128)(2,1)S(1)}, u32[]{:S(2)}, u32[]{:S(2)}) %collective-permute-start.8) | collective-permute-done | bytes 262176 | tf_op jit(solution)/shard_map/ppermute | solution.py:33
  21.1 2.4 collective-permute-start.9
  23.6 4.3 %collective-permute-start.2 = (bf16[8,256,64]{1,2,0:T(8,128)(2,1)S(1)}, bf16[8,256,64]{1,2,0:T(8,128)(2,1)}, u32[]{:S(2)}, u32[]{:S(2)}) collective-permute-start(bf16[8,256,64]{1,2,0:T(8,128)(2,1)S(1)} %collective-permute-done.1), channel_id=1, source_target_pairs={{0,480},{32,0},{64,32},{96,64},{128,96},{160,128},{192,160},{224,1... | collective-permute-start | bytes 786440 | tf_op jit(solution)/shard_map/ppermute | solution.py:36
  27.9 2.7 collective-permute-done.9
  30.6 1.9 collective-permute-start.10
  32.6 4.9 %collective-permute-start.3 = (bf16[8,256,64]{1,2,0:T(8,128)(2,1)}, bf16[8,256,64]{1,2,0:T(8,128)(2,1)}, u32[]{:S(2)}, u32[]{:S(2)}) collective-permute-start(bf16[8,256,64]{1,2,0:T(8,128)(2,1)} %collective-permute-done.2), channel_id=1, source_target_pairs={{0,480},{32,0},{64,32},{96,64},{128,96},{160,128},{192,160},{224,1... | collective-permute-start | bytes 786440 | tf_op jit(solution)/shard_map/ppermute | solution.py:36
  37.5 3.9 %copy.53 = bf16[16,2,8,24,256]{4,3,2,0,1:T(8,128)(2,1)} copy(bf16[16,2,8,24,256]{4,3,2,1,0:T(8,128)(2,1)} %bitcast.283) | data formatting | bytes 6291456 | tf_op jit(solution)/shard_map/reshape;squeeze | solution.py:21
  41.3 3.9 %all-to-all-start = ((bf16[16,2,8,24,256]{4,3,2,0,1:T(8,128)(2,1)}), bf16[16,2,8,24,256]{4,3,2,0,1:T(8,128)(2,1)S(1)}, u32[]{:S(2)}, u32[]{:S(2)}) async-start(bf16[16,2,8,24,256]{4,3,2,0,1:T(8,128)(2,1)} %copy.53), calls=%async_computation | async-start | bytes 6291456 | tf_op jit(solution)/shard_map/all_to_all | solution.py:22
  45.3 3.6 %all-to-all-done = bf16[16,2,8,24,256]{4,3,2,0,1:T(8,128)(2,1)S(1)} async-done(((bf16[16,2,8,24,256]{4,3,2,0,1:T(8,128)(2,1)}), bf16[16,2,8,24,256]{4,3,2,0,1:T(8,128)(2,1)S(1)}, u32[]{:S(2)}, u32[]{:S(2)}) %all-to-all-start) | async-done | bytes 3145760 | tf_op jit(solution)/shard_map/all_to_all | solution.py:22
  49.2 1.9 collective-permute-start.11
  52.0 5.4 %collective-permute-start.4 = (bf16[8,256,64]{1,2,0:T(8,128)(2,1)}, bf16[8,256,64]{1,2,0:T(8,128)(2,1)S(1)}, u32[]{:S(2)}, u32[]{:S(2)}) collective-permute-start(bf16[8,256,64]{1,2,0:T(8,128)(2,1)} %collective-permute-done.3), channel_id=1, source_target_pairs={{0,480},{32,0},{64,32},{96,64},{128,96},{160,128},{192,160},{224,1... | collective-permute-start | bytes 786440 | tf_op jit(solution)/shard_map/ppermute | solution.py:36
  57.4 1.9 constant_dynamic-update-slice_fusion.30
  59.3 2.0 collective-permute-done.11
  61.2 1.9 collective-permute-start.12
  63.2 1.9 constant_dynamic-update-slice_fusion.29
  65.1 4.8 %collective-permute-start.5 = (bf16[8,256,64]{1,2,0:T(8,128)(2,1)S(1)}, bf16[8,256,64]{1,2,0:T(8,128)(2,1)S(1)}, u32[]{:S(2)}, u32[]{:S(2)}) collective-permute-start(bf16[8,256,64]{1,2,0:T(8,128)(2,1)S(1)} %collective-permute-done.4), channel_id=1, source_target_pairs={{0,480},{32,0},{64,32},{96,64},{128,96},{160,128},{192,160},{224,1... | collective-permute-start | bytes 786440 | tf_op jit(solution)/shard_map/ppermute | solution.py:36
  69.9 1.9 constant_dynamic-update-slice_fusion.28
  72.0 1.9 collective-permute-start.13
  74.0 1.9 constant_dynamic-update-slice_fusion.27
  75.9 4.9 %collective-permute-start.6 = (bf16[8,256,64]{1,2,0:T(8,128)(2,1)S(1)}, bf16[8,256,64]{1,2,0:T(8,128)(2,1)S(1)}, u32[]{:S(2)}, u32[]{:S(2)}) collective-permute-start(bf16[8,256,64]{1,2,0:T(8,128)(2,1)S(1)} %collective-permute-done.5), channel_id=1, source_target_pairs={{0,480},{32,0},{64,32},{96,64},{128,96},{160,128},{192,160},{224,1... | collective-permute-start | bytes 786440 | tf_op jit(solution)/shard_map/ppermute | solution.py:36
  80.9 1.8 constant_dynamic-update-slice_fusion.26
  82.7 1.9 collective-permute-start.14
  86.3 6.1 %collective-permute-done.14 = bf16[8,256,64]{1,2,0:T(8,128)(2,1)S(1)} collective-permute-done((bf16[8,256,64]{1,2,0:T(8,128)(2,1)S(1)}, bf16[8,256,64]{1,2,0:T(8,128)(2,1)S(1)}, u32[]{:S(2)}, u32[]{:S(2)}) %collective-permute-start.14) | collective-permute-done | bytes 262176 | tf_op jit(solution)/shard_map/ppermute | solution.py:33
  95.0 1.8 constant_dynamic-update-slice_fusion.20
  96.8 1.8 constant_dynamic-update-slice_fusion.19
  98.6 1.8 constant_dynamic-update-slice_fusion.18
  112.5 1.5 fusion.95
  114.1 1.9 reshape.225
  116.0 13.5 %all-to-all-start.1 = ((bf16[16,2,12288]{2,1,0:T(2,128)(2,1)}), bf16[16,2,12288]{2,1,0:T(2,128)(2,1)S(1)}, u32[]{:S(2)}, u32[]{:S(2)}) async-start(bf16[16,2,12288]{2,1,0:T(2,128)(2,1)} %reshape.225), calls=%async_computation.1 | async-start | bytes 1572864 | tf_op jit(solution)/shard_map/all_to_all | solution.py:49
  130.6 30.8 %all-to-all-done.1 = bf16[16,2,12288]{2,1,0:T(2,128)(2,1)S(1)} async-done(((bf16[16,2,12288]{2,1,0:T(2,128)(2,1)}), bf16[16,2,12288]{2,1,0:T(2,128)(2,1)S(1)}, u32[]{:S(2)}, u32[]{:S(2)}) %all-to-all-start.1) | async-done | bytes 786464 | tf_op jit(solution)/shard_map/all_to_all | solution.py:49
  161.3 1.0 reshape.226
  162.6 1.5 copy.56
  164.1 4.9 %convolution_convert_fusion = bf16[16,3,392,128]{3,0,2,1:T(8,128)(2,1)S(1)} fusion(bf16[8,1,6]{2,0,1:T(8,128)(2,1)S(1)} %get-tuple-element.8, bf16[8,1,6]{2,0,1:T(8,128)(2,1)S(1)} %get-tuple-element.7, bf16[8,384,128]{2,0,1:T(8,128)(2,1)} %bitcast.284, bf16[392]{0:T(512)(128)(2,1)S(1)} %pad.4.clone, bf16[392,128]{1,0:T(8,128)(2,1)S(1)} %pad.3.clone, ...), kind=kOutput, calls=%fused_computation | convolution fusion | flops 44957696 | bytes 5705424 | tf_op jit(solution)/shard_map/dsk,kyp->dsyp/dot_general | solution.py:77
  169.0 3.4 %copy.57 = bf16[16,3,392,128]{3,2,1,0:T(8,128)(2,1)} copy(bf16[16,3,392,128]{3,0,2,1:T(8,128)(2,1)S(1)} %convolution_convert_fusion) | data formatting | bytes 9633792 | tf_op jit(solution)/shard_map/convert_element_type | solution.py:77
  172.4 7.1 %all-to-all-start.2 = ((bf16[16,3,392,128]{3,2,1,0:T(8,128)(2,1)}), bf16[16,3,392,128]{3,2,1,0:T(8,128)(2,1)}, u32[]{:S(2)}, u32[]{:S(2)}) async-start(bf16[16,3,392,128]{3,2,1,0:T(8,128)(2,1)} %copy.57), calls=%async_computation.2 | async-start | bytes 9633792 | tf_op jit(solution)/shard_map/all_to_all | solution.py:80
  179.6 3.1 %copy.60 = bf16[1,8,64,16,48]{4,3,2,1,0:T(8,128)(2,1)} copy(bf16[1,8,64,16,48]{2,4,1,3,0:T(8,128)(2,1)S(1)} %bitcast_bitcast_fusion) | data formatting | bytes 1572864 | tf_op jit(solution)/shard_map/all_to_all | solution.py:49
  182.7 4.3 %squeeze.84.own_ref = bf16[8,64,768]{2,1,0:T(8,128)(2,1)} reshape(bf16[1,8,64,16,48]{4,3,2,1,0:T(8,128)(2,1)} %copy.60) | data formatting | bytes 1572864 | tf_op jit(solution)/shard_map/squeeze | solution.py:49
  187.0 69.8 %all-to-all-done.2 = bf16[16,3,392,128]{3,2,1,0:T(8,128)(2,1)} async-done(((bf16[16,3,392,128]{3,2,1,0:T(8,128)(2,1)}), bf16[16,3,392,128]{3,2,1,0:T(8,128)(2,1)}, u32[]{:S(2)}, u32[]{:S(2)}) %all-to-all-start.2) | async-done | bytes 4816928 | tf_op jit(solution)/shard_map/all_to_all | solution.py:80
  256.8 0.9 slice.12
  259.0 19.0 %shard_map.46 = bf16[8,64,1536]{2,1,0:T(8,128)(2,1)} custom-call(s32[24]{0:T(128)} %copy-done.11, s32[1152]{0:T(1024)} %sub.25.eidx_ref, bf16[8,64,768]{2,1,0:T(8,128)(2,1)} %squeeze.84.own_ref, bf16[48,392,128]{2,1,0:T(8,128)(2,1)} %bitcast.69.recv_ref), custom_call_target="tpu_custom_call" | custom-call | tf_op jit(solution)/shard_map/pallas_call | solution.py:121
  278.0 4.0 %reshape.221 = bf16[8,64,24,64]{3,2,1,0:T(8,128)(2,1)S(1)} reshape(bf16[8,64,1536]{2,1,0:T(8,128)(2,1)} %shard_map.46) | data formatting | bytes 3145728 | tf_op jit(solution)/shard_map/reshape | solution.py:92
  282.0 2.5 copy.61
  284.5 5.2 %reshape.222 = bf16[1,8,24,4096]{3,2,1,0:T(8,128)(2,1)} reshape(bf16[8,24,64,64]{3,2,1,0:T(8,128)(2,1)} %copy.61) | data formatting | bytes 3145728 | tf_op jit(solution)/shard_map/reshape | solution.py:93
  (86 shorter events, 21.8 us)
Async XLA Ops:
  0.0 10.1 %collective-permute-start.7 = (bf16[8,256,64]{1,2,0:T(8,128)(2,1)}, bf16[8,256,64]{1,2,0:T(8,128)(2,1)S(1)}, u32[]{:S(2)}, u32[]{:S(2)}) collective-permute-start(bf16[8,256,64]{1,2,0:T(8,128)(2,1)} %bitcast.285), channel_id=1, source_target_pairs={{0,32},{32,64},{64,96},{96,128},{128,160},{160,192},{192,224},{224... | collective-permute-start | bytes 786440 | tf_op jit(solution)/shard_map/ppermute | solution.py:33
  2.9 10.8 %collective-permute-start = (bf16[8,256,64]{1,2,0:T(8,128)(2,1)}, bf16[8,256,64]{1,2,0:T(8,128)(2,1)S(1)}, u32[]{:S(2)}, u32[]{:S(2)}) collective-permute-start(bf16[8,256,64]{1,2,0:T(8,128)(2,1)} %bitcast.286), channel_id=1, source_target_pairs={{0,480},{32,0},{64,32},{96,64},{128,96},{160,128},{192,160},{224,1... | collective-permute-start | bytes 786440 | tf_op jit(solution)/shard_map/ppermute | solution.py:36
  10.1 0.7 copy-start.3
  10.8 9.6 %collective-permute-start.8 = (bf16[8,256,64]{1,2,0:T(8,128)(2,1)S(1)}, bf16[8,256,64]{1,2,0:T(8,128)(2,1)S(1)}, u32[]{:S(2)}, u32[]{:S(2)}) collective-permute-start(bf16[8,256,64]{1,2,0:T(8,128)(2,1)S(1)} %collective-permute-done.7), channel_id=1, source_target_pairs={{0,32},{32,64},{64,96},{96,128},{128,160},{160,192},{192,224},{224... | collective-permute-start | bytes 786440 | tf_op jit(solution)/shard_map/ppermute | solution.py:33
  13.8 16.9 %copy-start.7 = (bf16[8,256,64]{1,2,0:T(8,128)(2,1)}, bf16[8,256,64]{1,2,0:T(8,128)(2,1)S(1)}, u32[]{:S(2)}) copy-start(bf16[8,256,64]{1,2,0:T(8,128)(2,1)S(1)} %collective-permute-done) | copy-start | bytes 786436
  13.8 9.8 %collective-permute-start.1 = (bf16[8,256,64]{1,2,0:T(8,128)(2,1)S(1)}, bf16[8,256,64]{1,2,0:T(8,128)(2,1)S(1)}, u32[]{:S(2)}, u32[]{:S(2)}) collective-permute-start(bf16[8,256,64]{1,2,0:T(8,128)(2,1)S(1)} %collective-permute-done), channel_id=1, source_target_pairs={{0,480},{32,0},{64,32},{96,64},{128,96},{160,128},{192,160},{224,1... | collective-permute-start | bytes 786440 | tf_op jit(solution)/shard_map/ppermute | solution.py:36
  20.4 0.7 copy-start.5
  21.1 9.5 %collective-permute-start.9 = (bf16[8,256,64]{1,2,0:T(8,128)(2,1)S(1)}, bf16[8,256,64]{1,2,0:T(8,128)(2,1)}, u32[]{:S(2)}, u32[]{:S(2)}) collective-permute-start(bf16[8,256,64]{1,2,0:T(8,128)(2,1)S(1)} %collective-permute-done.8), channel_id=1, source_target_pairs={{0,32},{32,64},{64,96},{96,128},{128,160},{160,192},{192,224},{224... | collective-permute-start | bytes 786440 | tf_op jit(solution)/shard_map/ppermute | solution.py:33
  23.5 9.0 %copy-start.8 = (bf16[8,256,64]{1,2,0:T(8,128)(2,1)}, bf16[8,256,64]{1,2,0:T(8,128)(2,1)S(1)}, u32[]{:S(2)}) copy-start(bf16[8,256,64]{1,2,0:T(8,128)(2,1)S(1)} %collective-permute-done.1) | copy-start | bytes 786436
  23.6 9.0 %collective-permute-start.2 = (bf16[8,256,64]{1,2,0:T(8,128)(2,1)S(1)}, bf16[8,256,64]{1,2,0:T(8,128)(2,1)}, u32[]{:S(2)}, u32[]{:S(2)}) collective-permute-start(bf16[8,256,64]{1,2,0:T(8,128)(2,1)S(1)} %collective-permute-done.1), channel_id=1, source_target_pairs={{0,480},{32,0},{64,32},{96,64},{128,96},{160,128},{192,160},{224,1... | collective-permute-start | bytes 786440 | tf_op jit(solution)/shard_map/ppermute | solution.py:36
  30.6 18.6 %collective-permute-start.10 = (bf16[8,256,64]{1,2,0:T(8,128)(2,1)}, bf16[8,256,64]{1,2,0:T(8,128)(2,1)}, u32[]{:S(2)}, u32[]{:S(2)}) collective-permute-start(bf16[8,256,64]{1,2,0:T(8,128)(2,1)} %collective-permute-done.9), channel_id=1, source_target_pairs={{0,32},{32,64},{64,96},{96,128},{128,160},{160,192},{192,224},{224... | collective-permute-start | bytes 786440 | tf_op jit(solution)/shard_map/ppermute | solution.py:33
  32.6 19.4 %collective-permute-start.3 = (bf16[8,256,64]{1,2,0:T(8,128)(2,1)}, bf16[8,256,64]{1,2,0:T(8,128)(2,1)}, u32[]{:S(2)}, u32[]{:S(2)}) collective-permute-start(bf16[8,256,64]{1,2,0:T(8,128)(2,1)} %collective-permute-done.2), channel_id=1, source_target_pairs={{0,480},{32,0},{64,32},{96,64},{128,96},{160,128},{192,160},{224,1... | collective-permute-start | bytes 786440 | tf_op jit(solution)/shard_map/ppermute | solution.py:36
  41.3 7.6 %all-to-all-start = ((bf16[16,2,8,24,256]{4,3,2,0,1:T(8,128)(2,1)}), bf16[16,2,8,24,256]{4,3,2,0,1:T(8,128)(2,1)S(1)}, u32[]{:S(2)}, u32[]{:S(2)}) async-start(bf16[16,2,8,24,256]{4,3,2,0,1:T(8,128)(2,1)} %copy.53), calls=%async_computation | async-start | bytes 6291456 | tf_op jit(solution)/shard_map/all_to_all | solution.py:22
  45.3 5.8 %copy-start.2 = (bf16[1,8,256,64]{2,3,1,0:T(8,128)(2,1)S(1)}, bf16[1,8,256,64]{2,3,1,0:T(8,128)(2,1)}, u32[]{:S(2)}) copy-start(bf16[1,8,256,64]{2,3,1,0:T(8,128)(2,1)} %param.5) | copy-start | bytes 786436
  49.2 2.0 copy-start
  49.2 12.0 %collective-permute-start.11 = (bf16[8,256,64]{1,2,0:T(8,128)(2,1)}, bf16[8,256,64]{1,2,0:T(8,128)(2,1)}, u32[]{:S(2)}, u32[]{:S(2)}) collective-permute-start(bf16[8,256,64]{1,2,0:T(8,128)(2,1)} %collective-permute-done.10), channel_id=1, source_target_pairs={{0,32},{32,64},{64,96},{96,128},{128,160},{160,192},{192,224},{224... | collective-permute-start | bytes 786440 | tf_op jit(solution)/shard_map/ppermute | solution.py:33
  52.0 32.6 %copy-start.1 = (bf16[16,2,8,24,256]{4,3,1,2,0:T(8,128)(2,1)S(1)}, bf16[16,2,8,24,256]{4,3,1,2,0:T(8,128)(2,1)}, u32[]{:S(2)}) copy-start(bf16[16,2,8,24,256]{4,3,1,2,0:T(8,128)(2,1)} %copy-done) | copy-start | bytes 9437188
  52.0 13.1 %collective-permute-start.4 = (bf16[8,256,64]{1,2,0:T(8,128)(2,1)}, bf16[8,256,64]{1,2,0:T(8,128)(2,1)S(1)}, u32[]{:S(2)}, u32[]{:S(2)}) collective-permute-start(bf16[8,256,64]{1,2,0:T(8,128)(2,1)} %collective-permute-done.3), channel_id=1, source_target_pairs={{0,480},{32,0},{64,32},{96,64},{128,96},{160,128},{192,160},{224,1... | collective-permute-start | bytes 786440 | tf_op jit(solution)/shard_map/ppermute | solution.py:36
  61.2 10.8 %collective-permute-start.12 = (bf16[8,256,64]{1,2,0:T(8,128)(2,1)}, bf16[8,256,64]{1,2,0:T(8,128)(2,1)S(1)}, u32[]{:S(2)}, u32[]{:S(2)}) collective-permute-start(bf16[8,256,64]{1,2,0:T(8,128)(2,1)} %collective-permute-done.11), channel_id=1, source_target_pairs={{0,32},{32,64},{64,96},{96,128},{128,160},{160,192},{192,224},{224... | collective-permute-start | bytes 786440 | tf_op jit(solution)/shard_map/ppermute | solution.py:33
  65.1 10.8 %collective-permute-start.5 = (bf16[8,256,64]{1,2,0:T(8,128)(2,1)S(1)}, bf16[8,256,64]{1,2,0:T(8,128)(2,1)S(1)}, u32[]{:S(2)}, u32[]{:S(2)}) collective-permute-start(bf16[8,256,64]{1,2,0:T(8,128)(2,1)S(1)} %collective-permute-done.4), channel_id=1, source_target_pairs={{0,480},{32,0},{64,32},{96,64},{128,96},{160,128},{192,160},{224,1... | collective-permute-start | bytes 786440 | tf_op jit(solution)/shard_map/ppermute | solution.py:36
  72.0 10.6 %collective-permute-start.13 = (bf16[8,256,64]{1,2,0:T(8,128)(2,1)S(1)}, bf16[8,256,64]{1,2,0:T(8,128)(2,1)S(1)}, u32[]{:S(2)}, u32[]{:S(2)}) collective-permute-start(bf16[8,256,64]{1,2,0:T(8,128)(2,1)S(1)} %collective-permute-done.12), channel_id=1, source_target_pairs={{0,32},{32,64},{64,96},{96,128},{128,160},{160,192},{192,224},{224... | collective-permute-start | bytes 786440 | tf_op jit(solution)/shard_map/ppermute | solution.py:33
  74.0 26.4 %copy-start.6 = (bf16[8,256,64]{1,2,0:T(8,128)(2,1)S(1)}, bf16[8,256,64]{1,2,0:T(8,128)(2,1)}, u32[]{:S(2)}) copy-start(bf16[8,256,64]{1,2,0:T(8,128)(2,1)} %copy-done.5) | copy-start | bytes 786436
  75.9 9.6 %collective-permute-start.6 = (bf16[8,256,64]{1,2,0:T(8,128)(2,1)S(1)}, bf16[8,256,64]{1,2,0:T(8,128)(2,1)S(1)}, u32[]{:S(2)}, u32[]{:S(2)}) collective-permute-start(bf16[8,256,64]{1,2,0:T(8,128)(2,1)S(1)} %collective-permute-done.5), channel_id=1, source_target_pairs={{0,480},{32,0},{64,32},{96,64},{128,96},{160,128},{192,160},{224,1... | collective-permute-start | bytes 786440 | tf_op jit(solution)/shard_map/ppermute | solution.py:36
  80.8 20.4 %copy-start.4 = (bf16[8,256,64]{1,2,0:T(8,128)(2,1)S(1)}, bf16[8,256,64]{1,2,0:T(8,128)(2,1)}, u32[]{:S(2)}) copy-start(bf16[8,256,64]{1,2,0:T(8,128)(2,1)} %copy-done.3) | copy-start | bytes 786436
  82.7 9.7 %collective-permute-start.14 = (bf16[8,256,64]{1,2,0:T(8,128)(2,1)S(1)}, bf16[8,256,64]{1,2,0:T(8,128)(2,1)S(1)}, u32[]{:S(2)}, u32[]{:S(2)}) collective-permute-start(bf16[8,256,64]{1,2,0:T(8,128)(2,1)S(1)} %collective-permute-done.13), channel_id=1, source_target_pairs={{0,32},{32,64},{64,96},{96,128},{128,160},{160,192},{192,224},{224... | collective-permute-start | bytes 786440 | tf_op jit(solution)/shard_map/ppermute | solution.py:33
  112.5 17.0 %copy-start.9 = (s32[1,16,24]{2,1,0:T(8,128)S(1)}, s32[1,16,24]{2,1,0:T(8,128)}, u32[]{:S(2)}) copy-start(s32[1,16,24]{2,1,0:T(8,128)} %param.7) | copy-start | bytes 4612
  112.5 17.8 %copy-start.10 = (s32[1,8,6]{1,0,2:T(1,128)S(1)}, s32[1,8,6]{1,0,2:T(1,128)}, u32[]{:S(2)}) copy-start(s32[1,8,6]{1,0,2:T(1,128)} %param.6) | copy-start | bytes 580
  116.0 45.4 %all-to-all-start.1 = ((bf16[16,2,12288]{2,1,0:T(2,128)(2,1)}), bf16[16,2,12288]{2,1,0:T(2,128)(2,1)S(1)}, u32[]{:S(2)}, u32[]{:S(2)}) async-start(bf16[16,2,12288]{2,1,0:T(2,128)(2,1)} %reshape.225), calls=%async_computation.1 | async-start | bytes 1572864 | tf_op jit(solution)/shard_map/all_to_all | solution.py:49
  172.4 84.4 %all-to-all-start.2 = ((bf16[16,3,392,128]{3,2,1,0:T(8,128)(2,1)}), bf16[16,3,392,128]{3,2,1,0:T(8,128)(2,1)}, u32[]{:S(2)}, u32[]{:S(2)}) async-start(bf16[16,3,392,128]{3,2,1,0:T(8,128)(2,1)} %copy.57), calls=%async_computation.2 | async-start | bytes 9633792 | tf_op jit(solution)/shard_map/all_to_all | solution.py:80
  179.6 78.3 %copy-start.11 = (s32[24]{0:T(128)}, s32[24]{0:T(128)S(1)}, u32[]{:S(2)}) copy-start(s32[24]{0:T(128)S(1)} %fusion.92.slot_ref) | copy-start | bytes 292

commit v5 on v3

--- a/solution.py
+++ b/solution.py
@@ -65,53 +65,50 @@
     codes = recv[:, nblk * nosv, : 2 * FBLK].astype(jnp.float32)
     pcode = jnp.einsum("ns,sc->nc", pick, codes)
     pblocks = (pcode[:, :FBLK] * 8 + pcode[:, FBLK:]).astype(jnp.int32)
-    match = own_blocks[:, None, :, None] == pblocks[None, :, None, :]
-    eidx = jnp.sum(jnp.where(match, jnp.arange(1, FBLK + 1)[None, None, None, :], 0), axis=3) - 1
-    res = pair_call(slot, eidx.astype(jnp.int32).reshape(-1), projected, recv)
-    pair = res.reshape(n_loc, nosv, npart, nosv).transpose(0, 2, 1, 3)
+    match = pblocks[:, None, None, :] == own_blocks[None, :, :, None]
+    bidx = jnp.sum(jnp.where(match, jnp.arange(1, FBLK + 1)[None, None, :, None], 0), axis=2) - 1
+    pair = pair_call(slot, bidx.astype(jnp.int32).reshape(-1), blocks_major, recv)
     return pair.reshape(1, n_loc, npart, nosv * nosv)
 
 
-def pair_kernel(slot_ref, eidx_ref, own_ref, recv_ref, out_ref, a_ref, *, npart, nosv):
-    r = pl.program_id(0)
-
-    def fill(n, carry):
-        s = slot_ref[n]
-        for b in range(FBLK):
-            e = eidx_ref[(r * npart + n) * FBLK + b]
-            ee = jnp.maximum(e, 0)
-            blk = recv_ref[s, pl.ds(pl.multiple_of(ee * nosv, nosv), nosv), :]
-            blk = jnp.where(e >= 0, blk, jnp.zeros_like(blk))
-            a_ref[pl.ds(pl.multiple_of(n * nosv, nosv), nosv), pl.ds(b * BLK, BLK)] = blk
-        return carry
-
-    lax.fori_loop(0, npart, fill, 0)
+def pair_kernel(slot_ref, bidx_ref, own_ref, recv_ref, out_ref, al_ref):
+    n = pl.program_id(0)
+    n_loc, nblk, nosv, _ = own_ref.shape
+    s = slot_ref[n]
+    for r in range(n_loc):
+        for e in range(nblk):
+            b = bidx_ref[(n * n_loc + r) * nblk + e]
+            blk = own_ref[r, jnp.maximum(b, 0)]
+            blk = jnp.where(b >= 0, blk, jnp.zeros_like(blk))
+            al_ref[r * nosv : (r + 1) * nosv, e * BLK : (e + 1) * BLK] = blk
+    part = jnp.concatenate(
+        [recv_ref[s, e * nosv : (e + 1) * nosv, :] for e in range(nblk)], axis=1
+    )
     res = lax.dot_general(
-        own_ref[0], a_ref[...], (((1,), (1,)), ((), ())), preferred_element_type=jnp.float32
+        al_ref[...], part, (((1,), (1,)), ((), ())), preferred_element_type=jnp.float32
     )
-    out_ref[0] = res.astype(out_ref.dtype)
+    out_ref[:, 0] = res.reshape(n_loc, nosv, nosv).astype(out_ref.dtype)
 
 
-def pair_call(slot, eidx, own, recv, interpret=False):
-    n_loc, nosv, fd = own.shape
+def pair_call(slot, bidx, own_bm, recv, interpret=False):
+    n_loc, nblk, nosv, _ = own_bm.shape
     npart = slot.shape[0]
     nslot, rows, _ = recv.shape
-    kern = functools.partial(pair_kernel, npart=npart, nosv=nosv)
     return pl.pallas_call(
-        kern,
-        out_shape=jax.ShapeDtypeStruct((n_loc, nosv, npart * nosv), jnp.bfloat16),
+        pair_kernel,
+        out_shape=jax.ShapeDtypeStruct((n_loc, npart, nosv, nosv), jnp.bfloat16),
         grid_spec=pltpu.PrefetchScalarGridSpec(
             num_scalar_prefetch=2,
-            grid=(n_loc,),
+            grid=(npart,),
             in_specs=[
-                pl.BlockSpec((1, nosv, fd), lambda r, s, e: (r, 0, 0)),
-                pl.BlockSpec((nslot, rows, BLK), lambda r, s, e: (0, 0, 0)),
+                pl.BlockSpec((n_loc, nblk, nosv, BLK), lambda n, s, b: (0, 0, 0, 0)),
+                pl.BlockSpec((nslot, rows, BLK), lambda n, s, b: (0, 0, 0)),
             ],
-            out_specs=pl.BlockSpec((1, nosv, npart * nosv), lambda r, s, e: (r, 0, 0)),
-            scratch_shapes=[pltpu.VMEM((npart * nosv, fd), jnp.bfloat16)],
+            out_specs=pl.BlockSpec((n_loc, 1, nosv, nosv), lambda n, s, b: (0, n, 0, 0)),
+            scratch_shapes=[pltpu.VMEM((n_loc * nosv, nblk * BLK), jnp.bfloat16)],
         ),
         interpret=interpret,
-    )(slot, eidx, own, recv)
+    )(slot, bidx, own_bm, recv)
 
 
 def solution(mesh):

time: 256 us -> 246 us (0.961)
  local copies, waits for them, and re-layouts: 33.8 us -> 20.6 us
  waiting for transfers between devices: 156 us -> 162 us
    all_to_all x1, waiting for transfers between devices: 55.3 us -> 61.3 us  [per_device(): recv = lax.all_to_all(send, 'orb', split_axis=0, concat_axis=0, tiled=True)]
    squeeze x1, local copies, waits for them, and re-layouts: 4.3 us -> 0.01 us  [per_device(): own_blocks = fit_blocks[0]]
    transpose x2 -> x0, local copies, waits for them, and re-layouts: 4.02 us -> none  [the longest x1 2.53 us: per_device(): pair = res.reshape(n_loc, nosv, npart, nosv).transpose(0, 2, 1, 3)]
    reshape x1, local copies, waits for them, and re-layouts: 3.97 us -> 0.79 us  [per_device(): blocks_major.reshape(n_loc, nblk * nosv, BLK)]
    all_to_all x3 -> x2, local copies, waits for them, and re-layouts: 3.36 us -> 0.22 us  [per_device(): lax.all_to_all(part, 'z', split_axis=0, concat_axis=3, tiled=True)[0]]
  transfers between devices with their start and end apart: 3 -> 3, of which waited for: 3 -> 3; matrix products, arithmetic and copies ran while one was open for 4% -> 2% of each run, Pallas kernels for 0% -> 0%
where the time goes in v5:
time: 246 us; the launch traced here: 245 us
  waiting for transfers between devices  162 us (66%)
  local copies, waits for them, and re-layouts  20.6 us (8%)
  Pallas kernels  17 us (7%)
  starting transfers between devices  16 us (7%)
  between operations  13.5 us (5%)
  matrix products  8.67 us (4%)
  blocking collectives  6.26 us (3%)
    all_gather x1, waiting for transfers between devices, per_device(): coef = lax.all_gather(osv_coef[0], 'z', axis=0, tiled=False)  73.4 us
    all_to_all x1, waiting for transfers between devices, per_device(): recv = lax.all_to_all(send, 'orb', split_axis=0, concat_axis=0, tiled=True)  61.3 us
    all_to_all x1, waiting for transfers between devices, per_device(): lax.all_to_all(part, 'z', split_axis=0, concat_axis=3, tiled=True)[0]  27.1 us
    pallas_call x1, Pallas kernels, pair_call(): pl.pallas_call(pair_kernel, out_shape=jax.ShapeDtypeStruct((n_loc, npart,...  17 us
    all_to_all x1, starting transfers between devices, per_device(): lax.all_to_all(part, 'z', split_axis=0, concat_axis=3, tiled=True)[0]  8.77 us
    all_to_all x1, starting transfers between devices, per_device(): recv = lax.all_to_all(send, 'orb', split_axis=0, concat_axis=0, tiled=True)  7.23 us
    all_to_all x1, blocking collectives, per_device(): mine = lax.all_to_all(rows, 'core', split_axis=1, concat_axis=3, tiled=True)  6.26 us
    reshape x1, local copies, waits for them, and re-layouts, per_device(): return pair.reshape(1, n_loc, npart, nosv * nosv)  5.15 us
  transfers between devices with their start and end apart: 3, of which 3 were waited for; matrix products, arithmetic and copies ran while one was open for 2% of the time, Pallas kernels for 0%

profile of v5, /device:TPU:116, one launch (start us, length us, event | category | flops | bytes accessed | tf_op | source)
XLA Modules:
  0.0 245.3 jit_solution(14117949687884609485)
XLA Ops:
  6.5 0.0 all-gather.2.cloned.1.call-start
  6.5 0.7 all-gather.2.cloned.1.call-update
  7.3 2.2 copy.47
  9.5 6.3 %all_to_all.35 = bf16[16,2,8,24,256]{4,3,2,0,1:T(8,128)(2,1)S(1)} all-to-all(bf16[16,2,8,24,256]{4,3,2,0,1:T(8,128)(2,1)S(1)} %copy.47), channel_id=1, replica_groups=mesh['z'=16,'core'=2,'orb'=16] {'core'}, dimensions={1} | all-to-all | bytes 6291456 | tf_op jit(solution)/shard_map/all_to_all | solution.py:22
  15.7 0.3 copy.48
  16.0 73.4 %all-gather.2.cloned.1.call-done = bf16[16,8,256,64]{2,3,1,0:T(8,128)(2,1)} async-done(((bf16[1,8,256,64]{2,3,1,0:T(8,128)(2,1)}), bf16[16,8,256,64]{2,3,1,0:T(8,128)(2,1)}) %all-gather.2.cloned.1.call-update) | async-done | bytes 4194320 | tf_op jit(solution)/shard_map/all_gather | solution.py:24
  89.4 4.6 %fusion.27 = bf16[16,8,48,64]{3,2,1,0:T(8,128)(2,1)} fusion(bf16[16,8,256,64]{2,3,1,0:T(8,128)(2,1)} %all-gather.2.cloned.1.call-done, bf16[16,8,48,256]{3,2,1,0:T(8,128)(2,1)S(1)} %bitcast.101), kind=kOutput, calls=%fused_computation.60 | convolution fusion | flops 201719808 | bytes 8126464 | tf_op jit(solution)/shard_map/zkfm,zkma->zkaf/dot_general | solution.py:25
  93.9 0.0 copy-start.1
  94.0 0.0 copy-start
  94.0 3.9 %reshape.220 = bf16[16,2,12288]{2,1,0:T(2,128)(2,1)} reshape(bf16[16,8,48,64]{3,2,1,0:T(8,128)(2,1)} %fusion.27) | data formatting | bytes 1572864
  97.8 8.8 %all-to-all-start.1 = ((bf16[16,2,12288]{2,1,0:T(2,128)(2,1)}), bf16[16,2,12288]{2,1,0:T(2,128)(2,1)S(1)}, u32[]{:S(2)}, u32[]{:S(2)}) async-start(bf16[16,2,12288]{2,1,0:T(2,128)(2,1)} %reshape.220), calls=%async_computation.1 | async-start | bytes 1572864 | tf_op jit(solution)/shard_map/all_to_all | solution.py:28
  106.6 0.0 copy-done.1
  106.6 0.1 copy.51
  106.7 0.1 fusion.9
  106.7 0.0 copy-done
  106.8 0.4 select_reduce_fusion
  107.3 0.1 convert_reduce_fusion
  107.4 0.1 copy.46
  107.5 0.1 pad.4.clone
  107.6 0.1 pad.3.clone
  107.7 27.1 %all-to-all-done.1 = bf16[16,2,12288]{2,1,0:T(2,128)(2,1)S(1)} async-done(((bf16[16,2,12288]{2,1,0:T(2,128)(2,1)}), bf16[16,2,12288]{2,1,0:T(2,128)(2,1)S(1)}, u32[]{:S(2)}, u32[]{:S(2)}) %all-to-all-start.1) | async-done | bytes 786464 | tf_op jit(solution)/shard_map/all_to_all | solution.py:28
  134.8 1.0 reshape.221
  135.8 0.1 bitcast_bitcast_fusion
  135.9 0.1 copy.49
  136.0 0.8 copy.58
  136.8 3.9 %convolution_convert_fusion = bf16[16,3,392,128]{3,0,2,1:T(8,128)(2,1)S(1)} fusion(bf16[8,1,6]{2,0,1:T(8,128)(2,1)S(1)} %get-tuple-element.8, bf16[8,1,6]{2,0,1:T(8,128)(2,1)S(1)} %get-tuple-element.7, bf16[8,384,128]{2,0,1:T(8,128)(2,1)S(1)} %bitcast.105, bf16[392]{0:T(512)(128)(2,1)S(1)} %pad.4.clone, bf16[392,128]{1,0:T(8,128)(2,1)S(1)} %pad.3.clone, ...), kind=kOutput, calls=%fused_computation | convolution fusion | flops 44957696 | bytes 5705424 | tf_op jit(solution)/shard_map/dsk,kyp->dsyp/dot_general | solution.py:56
  140.7 3.4 %copy.53 = bf16[16,3,392,128]{3,2,1,0:T(8,128)(2,1)} copy(bf16[16,3,392,128]{3,0,2,1:T(8,128)(2,1)S(1)} %convolution_convert_fusion) | data formatting | bytes 9633792 | tf_op jit(solution)/shard_map/convert_element_type | solution.py:56
  144.2 7.2 %all-to-all-start.2 = ((bf16[16,3,392,128]{3,2,1,0:T(8,128)(2,1)}), bf16[16,3,392,128]{3,2,1,0:T(8,128)(2,1)}, u32[]{:S(2)}, u32[]{:S(2)}) async-start(bf16[16,3,392,128]{3,2,1,0:T(8,128)(2,1)} %copy.53), calls=%async_computation.2 | async-start | bytes 9633792 | tf_op jit(solution)/shard_map/all_to_all | solution.py:59
  151.4 0.0 copy-start.2
  151.4 1.4 copy.50
  152.8 61.3 %all-to-all-done.2 = bf16[16,3,392,128]{3,2,1,0:T(8,128)(2,1)} async-done(((bf16[16,3,392,128]{3,2,1,0:T(8,128)(2,1)}), bf16[16,3,392,128]{3,2,1,0:T(8,128)(2,1)}, u32[]{:S(2)}, u32[]{:S(2)}) %all-to-all-start.2) | async-done | bytes 4816928 | tf_op jit(solution)/shard_map/all_to_all | solution.py:59
  214.1 0.9 slice.12
  215.0 0.1 copy.54
  215.1 0.2 fusion.10
  215.3 0.1 select_reduce_fusion.1
  215.4 0.1 copy.56
  215.6 0.7 sub.21.bidx_ref
  216.3 0.0 copy-done.2
  216.3 17.0 %shard_map.46 = bf16[8,24,64,64]{3,2,1,0:T(8,128)(2,1)} custom-call(s32[24]{0:T(128)} %copy-done.2, s32[1152]{0:T(1024)} %sub.21.bidx_ref, bf16[8,6,64,128]{3,2,1,0:T(8,128)(2,1)} %bitcast.104, bf16[48,392,128]{2,1,0:T(8,128)(2,1)} %bitcast.18.recv_ref), custom_call_target="tpu_custom_call" | custom-call | tf_op jit(solution)/shard_map/pallas_call | solution.py:97
  233.3 5.2 %reshape.217 = bf16[1,8,24,4096]{3,2,1,0:T(8,128)(2,1)} reshape(bf16[8,24,64,64]{3,2,1,0:T(8,128)(2,1)} %shard_map.46) | data formatting | bytes 3145728 | tf_op jit(solution)/shard_map/reshape | solution.py:71
  (13 shorter events, 0.1 us)
Async XLA Ops:
  6.5 82.9 %all-gather.2.cloned.1.call-start = ((), (), s32[]{:S(2)}) async-start(), calls=%async_computation.3 | async-start | bytes 4456448 | tf_op jit(solution)/shard_map/all_gather | solution.py:24
  93.9 12.6 %copy-start.1 = (s32[1,8,6]{1,0,2:T(1,128)S(1)}, s32[1,8,6]{1,0,2:T(1,128)}, u32[]{:S(2)}) copy-start(s32[1,8,6]{1,0,2:T(1,128)} %param.6) | copy-start | bytes 580
  94.0 12.8 %copy-start = (s32[1,16,24]{2,1,0:T(8,128)S(1)}, s32[1,16,24]{2,1,0:T(8,128)}, u32[]{:S(2)}) copy-start(s32[1,16,24]{2,1,0:T(8,128)} %param.7) | copy-start | bytes 4612
  97.8 37.0 %all-to-all-start.1 = ((bf16[16,2,12288]{2,1,0:T(2,128)(2,1)}), bf16[16,2,12288]{2,1,0:T(2,128)(2,1)S(1)}, u32[]{:S(2)}, u32[]{:S(2)}) async-start(bf16[16,2,12288]{2,1,0:T(2,128)(2,1)} %reshape.220), calls=%async_computation.1 | async-start | bytes 1572864 | tf_op jit(solution)/shard_map/all_to_all | solution.py:28
  144.2 69.9 %all-to-all-start.2 = ((bf16[16,3,392,128]{3,2,1,0:T(8,128)(2,1)}), bf16[16,3,392,128]{3,2,1,0:T(8,128)(2,1)}, u32[]{:S(2)}, u32[]{:S(2)}) async-start(bf16[16,3,392,128]{3,2,1,0:T(8,128)(2,1)} %copy.53), calls=%async_computation.2 | async-start | bytes 9633792 | tf_op jit(solution)/shard_map/all_to_all | solution.py:59
  151.4 64.9 %copy-start.2 = (s32[24]{0:T(128)}, s32[24]{0:T(128)S(1)}, u32[]{:S(2)}) copy-start(s32[24]{0:T(128)S(1)} %add_bitcast_fusion.slot_ref) | copy-start | bytes 292
Sparse Core Ops, SparseCore 0:
  9.4 79.9 all-gather.1

commit v6 on v5

--- a/solution.py
+++ b/solution.py
@@ -71,44 +71,50 @@
     return pair.reshape(1, n_loc, npart, nosv * nosv)
 
 
-def pair_kernel(slot_ref, bidx_ref, own_ref, recv_ref, out_ref, al_ref):
-    n = pl.program_id(0)
-    n_loc, nblk, nosv, _ = own_ref.shape
-    s = slot_ref[n]
-    for r in range(n_loc):
-        for e in range(nblk):
-            b = bidx_ref[(n * n_loc + r) * nblk + e]
-            blk = own_ref[r, jnp.maximum(b, 0)]
-            blk = jnp.where(b >= 0, blk, jnp.zeros_like(blk))
-            al_ref[r * nosv : (r + 1) * nosv, e * BLK : (e + 1) * BLK] = blk
-    part = jnp.concatenate(
-        [recv_ref[s, e * nosv : (e + 1) * nosv, :] for e in range(nblk)], axis=1
-    )
-    res = lax.dot_general(
-        al_ref[...], part, (((1,), (1,)), ((), ())), preferred_element_type=jnp.float32
-    )
-    out_ref[:, 0] = res.reshape(n_loc, nosv, nosv).astype(out_ref.dtype)
+def make_pair_call(npb):
+    def pair_kernel(slot_ref, bidx_ref, own_ref, recv_ref, out_ref, al_ref):
+        g = pl.program_id(0)
+        n_loc, nblk, nosv, _ = own_ref.shape
+        for j in range(npb):
+            n = g * npb + j
+            s = slot_ref[n]
+            for r in range(n_loc):
+                for e in range(nblk):
+                    b = bidx_ref[(n * n_loc + r) * nblk + e]
+                    blk = own_ref[r, jnp.maximum(b, 0)]
+                    blk = jnp.where(b >= 0, blk, jnp.zeros_like(blk))
+                    al_ref[j, r * nosv : (r + 1) * nosv, e * BLK : (e + 1) * BLK] = blk
+            part = jnp.concatenate(
+                [recv_ref[s, e * nosv : (e + 1) * nosv, :] for e in range(nblk)], axis=1
+            )
+            res = lax.dot_general(
+                al_ref[j], part, (((1,), (1,)), ((), ())), preferred_element_type=jnp.float32
+            )
+            out_ref[:, j] = res.reshape(n_loc, nosv, nosv).astype(out_ref.dtype)
+
+    def pair_call(slot, bidx, own_bm, recv):
+        n_loc, nblk, nosv, _ = own_bm.shape
+        npart = slot.shape[0]
+        nslot, rows, _ = recv.shape
+        return pl.pallas_call(
+            pair_kernel,
+            out_shape=jax.ShapeDtypeStruct((n_loc, npart, nosv, nosv), jnp.bfloat16),
+            grid_spec=pltpu.PrefetchScalarGridSpec(
+                num_scalar_prefetch=2,
+                grid=(npart // npb,),
+                in_specs=[
+                    pl.BlockSpec((n_loc, nblk, nosv, BLK), lambda g, s, b: (0, 0, 0, 0)),
+                    pl.BlockSpec((nslot, rows, BLK), lambda g, s, b: (0, 0, 0)),
+                ],
+                out_specs=pl.BlockSpec((n_loc, npb, nosv, nosv), lambda g, s, b: (0, g, 0, 0)),
+                scratch_shapes=[pltpu.VMEM((npb, n_loc * nosv, nblk * BLK), jnp.bfloat16)],
+            ),
+        )(slot, bidx, own_bm, recv)
+
+    return pair_call
 
 
-def pair_call(slot, bidx, own_bm, recv, interpret=False):
-    n_loc, nblk, nosv, _ = own_bm.shape
-    npart = slot.shape[0]
-    nslot, rows, _ = recv.shape
-    return pl.pallas_call(
-        pair_kernel,
-        out_shape=jax.ShapeDtypeStruct((n_loc, npart, nosv, nosv), jnp.bfloat16),
-        grid_spec=pltpu.PrefetchScalarGridSpec(
-            num_scalar_prefetch=2,
-            grid=(npart,),
-            in_specs=[
-                pl.BlockSpec((n_loc, nblk, nosv, BLK), lambda n, s, b: (0, 0, 0, 0)),
-                pl.BlockSpec((nslot, rows, BLK), lambda n, s, b: (0, 0, 0)),
-            ],
-            out_specs=pl.BlockSpec((n_loc, 1, nosv, nosv), lambda n, s, b: (0, n, 0, 0)),
-            scratch_shapes=[pltpu.VMEM((n_loc * nosv, nblk * BLK), jnp.bfloat16)],
-        ),
-        interpret=interpret,
-    )(slot, bidx, own_bm, recv)
+pair_call = make_pair_call(4)
 
 
 def solution(mesh):

time: 246 us -> 241 us (0.980)
  Pallas kernels: 17 us -> 12.3 us
    pallas_call x1, Pallas kernels: 17 us -> 12.3 us  [pair_call(): pl.pallas_call(pair_kernel, out_shape=jax.ShapeDtypeStruct((n_loc, npart,...]
where the time goes in v6:
time: 241 us
  waiting for transfers between devices  162 us (67%)
  local copies, waits for them, and re-layouts  20.6 us (9%)
  starting transfers between devices  16 us (7%)
  between operations  13.5 us (6%)
  Pallas kernels  12.3 us (5%)
  matrix products  8.67 us (4%)
  blocking collectives  6.26 us (3%)
    all_gather x1, waiting for transfers between devices, per_device(): coef = lax.all_gather(osv_coef[0], 'z', axis=0, tiled=False)  73.4 us
    all_to_all x1, waiting for transfers between devices, per_device(): recv = lax.all_to_all(send, 'orb', split_axis=0, concat_axis=0, tiled=True)  61.3 us
    all_to_all x1, waiting for transfers between devices, per_device(): lax.all_to_all(part, 'z', split_axis=0, concat_axis=3, tiled=True)[0]  27.1 us
    pallas_call x1, Pallas kernels, pair_call(): pl.pallas_call(pair_kernel, out_shape=jax.ShapeDtypeStruct((n_loc, npart,...  12.3 us
    all_to_all x1, starting transfers between devices, per_device(): lax.all_to_all(part, 'z', split_axis=0, concat_axis=3, tiled=True)[0]  8.77 us
    all_to_all x1, starting transfers between devices, per_device(): recv = lax.all_to_all(send, 'orb', split_axis=0, concat_axis=0, tiled=True)  7.23 us
    all_to_all x1, blocking collectives, per_device(): mine = lax.all_to_all(rows, 'core', split_axis=1, concat_axis=3, tiled=True)  6.26 us
    reshape x1, local copies, waits for them, and re-layouts, per_device(): return pair.reshape(1, n_loc, npart, nosv * nosv)  5.15 us
  transfers between devices with their start and end apart: 3, of which 3 were waited for; matrix products, arithmetic and copies ran while one was open for 2% of the time, Pallas kernels for 0%

profile of v6, /device:TPU:116, one launch (start us, length us, event | category | flops | bytes accessed | tf_op | source)
XLA Modules:
  0.0 240.6 jit_solution(3314782009180691856)
XLA Ops:
  6.5 0.0 all-gather.2.cloned.1.call-start
  6.5 0.7 all-gather.2.cloned.1.call-update
  7.3 2.2 copy.47
  9.5 6.3 %all_to_all.35 = bf16[16,2,8,24,256]{4,3,2,0,1:T(8,128)(2,1)S(1)} all-to-all(bf16[16,2,8,24,256]{4,3,2,0,1:T(8,128)(2,1)S(1)} %copy.47), channel_id=1, replica_groups=mesh['z'=16,'core'=2,'orb'=16] {'core'}, dimensions={1} | all-to-all | bytes 6291456 | tf_op jit(solution)/shard_map/all_to_all | solution.py:22
  15.7 0.3 copy.48
  16.0 73.4 %all-gather.2.cloned.1.call-done = bf16[16,8,256,64]{2,3,1,0:T(8,128)(2,1)} async-done(((bf16[1,8,256,64]{2,3,1,0:T(8,128)(2,1)}), bf16[16,8,256,64]{2,3,1,0:T(8,128)(2,1)}) %all-gather.2.cloned.1.call-update) | async-done | bytes 4194320 | tf_op jit(solution)/shard_map/all_gather | solution.py:24
  89.4 4.6 %fusion.27 = bf16[16,8,48,64]{3,2,1,0:T(8,128)(2,1)} fusion(bf16[16,8,256,64]{2,3,1,0:T(8,128)(2,1)} %all-gather.2.cloned.1.call-done, bf16[16,8,48,256]{3,2,1,0:T(8,128)(2,1)S(1)} %bitcast.101), kind=kOutput, calls=%fused_computation.60 | convolution fusion | flops 201719808 | bytes 8126464 | tf_op jit(solution)/shard_map/zkfm,zkma->zkaf/dot_general | solution.py:25
  93.9 0.0 copy-start.1
  94.0 0.0 copy-start
  94.0 3.9 %reshape.220 = bf16[16,2,12288]{2,1,0:T(2,128)(2,1)} reshape(bf16[16,8,48,64]{3,2,1,0:T(8,128)(2,1)} %fusion.27) | data formatting | bytes 1572864
  97.8 8.8 %all-to-all-start.1 = ((bf16[16,2,12288]{2,1,0:T(2,128)(2,1)}), bf16[16,2,12288]{2,1,0:T(2,128)(2,1)S(1)}, u32[]{:S(2)}, u32[]{:S(2)}) async-start(bf16[16,2,12288]{2,1,0:T(2,128)(2,1)} %reshape.220), calls=%async_computation.1 | async-start | bytes 1572864 | tf_op jit(solution)/shard_map/all_to_all | solution.py:28
  106.6 0.0 copy-done.1
  106.6 0.1 copy.51
  106.7 0.1 fusion.9
  106.7 0.0 copy-done
  106.8 0.4 select_reduce_fusion
  107.3 0.1 convert_reduce_fusion
  107.4 0.1 copy.46
  107.5 0.1 pad.4.clone
  107.6 0.1 pad.3.clone
  107.7 27.1 %all-to-all-done.1 = bf16[16,2,12288]{2,1,0:T(2,128)(2,1)S(1)} async-done(((bf16[16,2,12288]{2,1,0:T(2,128)(2,1)}), bf16[16,2,12288]{2,1,0:T(2,128)(2,1)S(1)}, u32[]{:S(2)}, u32[]{:S(2)}) %all-to-all-start.1) | async-done | bytes 786464 | tf_op jit(solution)/shard_map/all_to_all | solution.py:28
  134.8 1.0 reshape.221
  135.8 0.1 bitcast_bitcast_fusion
  135.9 0.1 copy.49
  136.0 0.8 copy.58
  136.8 3.9 %convolution_convert_fusion = bf16[16,3,392,128]{3,0,2,1:T(8,128)(2,1)S(1)} fusion(bf16[8,1,6]{2,0,1:T(8,128)(2,1)S(1)} %get-tuple-element.8, bf16[8,1,6]{2,0,1:T(8,128)(2,1)S(1)} %get-tuple-element.7, bf16[8,384,128]{2,0,1:T(8,128)(2,1)S(1)} %bitcast.105, bf16[392]{0:T(512)(128)(2,1)S(1)} %pad.4.clone, bf16[392,128]{1,0:T(8,128)(2,1)S(1)} %pad.3.clone, ...), kind=kOutput, calls=%fused_computation | convolution fusion | flops 44957696 | bytes 5705424 | tf_op jit(solution)/shard_map/dsk,kyp->dsyp/dot_general | solution.py:56
  140.7 3.4 %copy.53 = bf16[16,3,392,128]{3,2,1,0:T(8,128)(2,1)} copy(bf16[16,3,392,128]{3,0,2,1:T(8,128)(2,1)S(1)} %convolution_convert_fusion) | data formatting | bytes 9633792 | tf_op jit(solution)/shard_map/convert_element_type | solution.py:56
  144.2 7.2 %all-to-all-start.2 = ((bf16[16,3,392,128]{3,2,1,0:T(8,128)(2,1)}), bf16[16,3,392,128]{3,2,1,0:T(8,128)(2,1)}, u32[]{:S(2)}, u32[]{:S(2)}) async-start(bf16[16,3,392,128]{3,2,1,0:T(8,128)(2,1)} %copy.53), calls=%async_computation.2 | async-start | bytes 9633792 | tf_op jit(solution)/shard_map/all_to_all | solution.py:59
  151.4 0.0 copy-start.2
  151.4 1.4 copy.50
  152.8 61.3 %all-to-all-done.2 = bf16[16,3,392,128]{3,2,1,0:T(8,128)(2,1)} async-done(((bf16[16,3,392,128]{3,2,1,0:T(8,128)(2,1)}), bf16[16,3,392,128]{3,2,1,0:T(8,128)(2,1)}, u32[]{:S(2)}, u32[]{:S(2)}) %all-to-all-start.2) | async-done | bytes 4816928 | tf_op jit(solution)/shard_map/all_to_all | solution.py:59
  214.1 0.9 slice.12
  215.0 0.1 copy.54
  215.1 0.2 fusion.10
  215.3 0.1 select_reduce_fusion.1
  215.4 0.1 copy.56
  215.6 0.7 sub.21.bidx_ref
  216.3 0.0 copy-done.2
  216.3 12.3 %shard_map.46 = bf16[8,24,64,64]{3,2,1,0:T(8,128)(2,1)} custom-call(s32[24]{0:T(128)} %copy-done.2, s32[1152]{0:T(1024)} %sub.21.bidx_ref, bf16[8,6,64,128]{3,2,1,0:T(8,128)(2,1)} %bitcast.104, bf16[48,392,128]{2,1,0:T(8,128)(2,1)} %bitcast.18.recv_ref), custom_call_target="tpu_custom_call" | custom-call | tf_op jit(solution)/shard_map/pallas_call | solution.py:99
  228.6 5.2 %reshape.217 = bf16[1,8,24,4096]{3,2,1,0:T(8,128)(2,1)} reshape(bf16[8,24,64,64]{3,2,1,0:T(8,128)(2,1)} %shard_map.46) | data formatting | bytes 3145728 | tf_op jit(solution)/shard_map/reshape | solution.py:71
  (13 shorter events, 0.1 us)
Async XLA Ops:
  6.5 82.9 %all-gather.2.cloned.1.call-start = ((), (), s32[]{:S(2)}) async-start(), calls=%async_computation.3 | async-start | bytes 4456448 | tf_op jit(solution)/shard_map/all_gather | solution.py:24
  93.9 12.6 %copy-start.1 = (s32[1,8,6]{1,0,2:T(1,128)S(1)}, s32[1,8,6]{1,0,2:T(1,128)}, u32[]{:S(2)}) copy-start(s32[1,8,6]{1,0,2:T(1,128)} %param.6) | copy-start | bytes 580
  94.0 12.8 %copy-start = (s32[1,16,24]{2,1,0:T(8,128)S(1)}, s32[1,16,24]{2,1,0:T(8,128)}, u32[]{:S(2)}) copy-start(s32[1,16,24]{2,1,0:T(8,128)} %param.7) | copy-start | bytes 4612
  97.8 37.0 %all-to-all-start.1 = ((bf16[16,2,12288]{2,1,0:T(2,128)(2,1)}), bf16[16,2,12288]{2,1,0:T(2,128)(2,1)S(1)}, u32[]{:S(2)}, u32[]{:S(2)}) async-start(bf16[16,2,12288]{2,1,0:T(2,128)(2,1)} %reshape.220), calls=%async_computation.1 | async-start | bytes 1572864 | tf_op jit(solution)/shard_map/all_to_all | solution.py:28
  144.2 69.9 %all-to-all-start.2 = ((bf16[16,3,392,128]{3,2,1,0:T(8,128)(2,1)}), bf16[16,3,392,128]{3,2,1,0:T(8,128)(2,1)}, u32[]{:S(2)}, u32[]{:S(2)}) async-start(bf16[16,3,392,128]{3,2,1,0:T(8,128)(2,1)} %copy.53), calls=%async_computation.2 | async-start | bytes 9633792 | tf_op jit(solution)/shard_map/all_to_all | solution.py:59
  151.4 64.9 %copy-start.2 = (s32[24]{0:T(128)}, s32[24]{0:T(128)S(1)}, u32[]{:S(2)}) copy-start(s32[24]{0:T(128)S(1)} %add_bitcast_fusion.slot_ref) | copy-start | bytes 292
Sparse Core Ops, SparseCore 0:
  9.4 79.9 all-gather.1

commit v7 on v6

--- a/solution.py
+++ b/solution.py
@@ -53,9 +53,8 @@
     )
     blocks_major = projected.reshape(n_loc, nosv, nblk, BLK).transpose(0, 2, 1, 3)
     payload = jnp.concatenate([blocks_major.reshape(n_loc, nblk * nosv, BLK), code], axis=1)
-    send = jnp.einsum("dsk,kyp->dsyp", sel, payload, preferred_element_type=jnp.float32).astype(
-        jnp.bfloat16
-    )
+    which = jnp.sum(sel.astype(jnp.int32) * jnp.arange(n_loc)[None, None, :], axis=2)
+    send = jnp.take(payload, which.reshape(-1), axis=0, mode="clip").reshape(ngroups, CAP, *payload.shape[1:])
     recv = lax.all_to_all(send, "orb", split_axis=0, concat_axis=0, tiled=True)
     recv = recv.reshape(ngroups * CAP, nblk * nosv + code_rows, BLK)
     my_owner = lax.dynamic_index_in_dim(owner, me, 0, keepdims=False)

time: 241 us -> 238 us (0.988)
  matrix products: 8.67 us -> 4.75 us
    dot_general x1 -> x0, matrix products: 3.91 us -> none  [per_device(): jnp.einsum('dsk,kyp->dsyp', sel, payload, preferred_element_type=jnp.floa...]
    gather x0 -> x1, local copies, waits for them, and re-layouts: none -> 3.57 us  [per_device(): jnp.take(payload, which.reshape(-1), axis=0, mode='clip')]
    convert_element_type x1 -> x0, local copies, waits for them, and re-layouts: 3.45 us -> none  [per_device(): jnp.einsum('dsk,kyp->dsyp', sel, payload, preferred_element_type=jnp.floa...]
    unnamed x9 -> x11, local copies, waits for them, and re-layouts: 4.95 us -> 4.95 us
where the time goes in v7:
time: 238 us; the launch traced here: 237 us
  waiting for transfers between devices  164 us (69%)
  local copies, waits for them, and re-layouts  19.4 us (8%)
  starting transfers between devices  16 us (7%)
  between operations  13.6 us (6%)
  Pallas kernels  12.3 us (5%)
  blocking collectives  6.26 us (3%)
  matrix products  4.75 us (2%)
    all_gather x1, waiting for transfers between devices, per_device(): coef = lax.all_gather(osv_coef[0], 'z', axis=0, tiled=False)  73.4 us
    all_to_all x1, waiting for transfers between devices, per_device(): recv = lax.all_to_all(send, 'orb', split_axis=0, concat_axis=0, tiled=True)  62.7 us
    all_to_all x1, waiting for transfers between devices, per_device(): lax.all_to_all(part, 'z', split_axis=0, concat_axis=3, tiled=True)[0]  26.8 us
    pallas_call x1, Pallas kernels, pair_call(): pl.pallas_call(pair_kernel, out_shape=jax.ShapeDtypeStruct((n_loc, npart,...  12.3 us
    all_to_all x1, starting transfers between devices, per_device(): lax.all_to_all(part, 'z', split_axis=0, concat_axis=3, tiled=True)[0]  8.77 us
    all_to_all x1, starting transfers between devices, per_device(): recv = lax.all_to_all(send, 'orb', split_axis=0, concat_axis=0, tiled=True)  7.23 us
    all_to_all x1, blocking collectives, per_device(): mine = lax.all_to_all(rows, 'core', split_axis=1, concat_axis=3, tiled=True)  6.26 us
    reshape x1, local copies, waits for them, and re-layouts, per_device(): return pair.reshape(1, n_loc, npart, nosv * nosv)  5.15 us
  transfers between devices with their start and end apart: 3, of which 3 were waited for; matrix products, arithmetic and copies ran while one was open for 2% of the time, Pallas kernels for 0%

profile of v7, /device:TPU:116, one launch (start us, length us, event | category | flops | bytes accessed | tf_op | source)
XLA Modules:
  0.0 237.0 jit_solution(16352628758143334665)
XLA Ops:
  6.5 0.0 all-gather.2.cloned.1.call-start
  6.5 0.7 all-gather.2.cloned.1.call-update
  7.3 2.2 copy.47
  9.5 6.3 %all_to_all.35 = bf16[16,2,8,24,256]{4,3,2,0,1:T(8,128)(2,1)S(1)} all-to-all(bf16[16,2,8,24,256]{4,3,2,0,1:T(8,128)(2,1)S(1)} %copy.47), channel_id=1, replica_groups=mesh['z'=16,'core'=2,'orb'=16] {'core'}, dimensions={1} | all-to-all | bytes 6291456 | tf_op jit(solution)/shard_map/all_to_all | solution.py:22
  15.7 0.3 copy.48
  16.0 73.4 %all-gather.2.cloned.1.call-done = bf16[16,8,256,64]{2,3,1,0:T(8,128)(2,1)} async-done(((bf16[1,8,256,64]{2,3,1,0:T(8,128)(2,1)}), bf16[16,8,256,64]{2,3,1,0:T(8,128)(2,1)}) %all-gather.2.cloned.1.call-update) | async-done | bytes 4194320 | tf_op jit(solution)/shard_map/all_gather | solution.py:24
  89.4 4.6 %fusion.16 = bf16[16,8,48,64]{3,2,1,0:T(8,128)(2,1)} fusion(bf16[16,8,256,64]{2,3,1,0:T(8,128)(2,1)} %all-gather.2.cloned.1.call-done, bf16[16,8,48,256]{3,2,1,0:T(8,128)(2,1)S(1)} %bitcast.93), kind=kOutput, calls=%fused_computation.51 | convolution fusion | flops 201719808 | bytes 8126464 | tf_op jit(solution)/shard_map/zkfm,zkma->zkaf/dot_general | solution.py:25
  93.9 0.0 copy-start.1
  94.0 0.0 copy-start.2
  94.0 3.9 %reshape.233 = bf16[16,2,12288]{2,1,0:T(2,128)(2,1)} reshape(bf16[16,8,48,64]{3,2,1,0:T(8,128)(2,1)} %fusion.16) | data formatting | bytes 1572864
  97.8 8.8 %all-to-all-start.1 = ((bf16[16,2,12288]{2,1,0:T(2,128)(2,1)}), bf16[16,2,12288]{2,1,0:T(2,128)(2,1)S(1)}, u32[]{:S(2)}, u32[]{:S(2)}) async-start(bf16[16,2,12288]{2,1,0:T(2,128)(2,1)} %reshape.233), calls=%async_computation.1 | async-start | bytes 1572864 | tf_op jit(solution)/shard_map/all_to_all | solution.py:28
  106.6 0.1 fusion.1
  106.7 0.0 copy-done.1
  106.7 0.4 select_reduce_fusion
  107.2 0.1 convert_reduce_fusion
  107.3 0.1 copy.54
  107.4 0.1 copy.55
  107.5 0.1 reshape.226
  107.6 0.0 copy-done.2
  107.6 0.1 copy.51
  107.8 0.1 pad.3.clone
  107.8 0.1 pad.4.clone
  107.9 26.8 %all-to-all-done.1 = bf16[16,2,12288]{2,1,0:T(2,128)(2,1)S(1)} async-done(((bf16[16,2,12288]{2,1,0:T(2,128)(2,1)}), bf16[16,2,12288]{2,1,0:T(2,128)(2,1)S(1)}, u32[]{:S(2)}, u32[]{:S(2)}) %all-to-all-start.1) | async-done | bytes 786464 | tf_op jit(solution)/shard_map/all_to_all | solution.py:28
  134.8 1.0 reshape.234
  135.8 0.1 bitcast_bitcast_fusion
  135.9 0.1 copy.49
  136.0 0.7 copy.50
  136.7 0.0 copy-start
  136.8 0.2 maximum_maximum_fusion
  137.0 3.6 %gather_fusion = bf16[48,392,128]{2,1,0:T(8,128)(2,1)} fusion(bf16[8,392,128]{2,1,0:T(8,128)(2,1)S(1)} %maximum_maximum_fusion, s32[1024]{0:T(1024)S(1)} %pad_clamp_fusion), kind=kCustom, calls=%fused_computation | custom fusion | bytes 9633984 | tf_op jit(solution)/shard_map/jit(_take)/gather | solution.py:57
  140.6 0.0 copy-done
  140.6 7.2 %all-to-all-start.2 = ((bf16[16,3,392,128]{3,2,1,0:T(8,128)(2,1)}), bf16[16,3,392,128]{3,2,1,0:T(8,128)(2,1)}, u32[]{:S(2)}, u32[]{:S(2)}) async-start(bf16[16,3,392,128]{3,2,1,0:T(8,128)(2,1)} %bitcast.92), calls=%async_computation.2 | async-start | bytes 9633792 | tf_op jit(solution)/shard_map/all_to_all | solution.py:58
  147.8 0.0 copy-start.3
  147.9 62.7 %all-to-all-done.2 = bf16[16,3,392,128]{3,2,1,0:T(8,128)(2,1)} async-done(((bf16[16,3,392,128]{3,2,1,0:T(8,128)(2,1)}), bf16[16,3,392,128]{3,2,1,0:T(8,128)(2,1)}, u32[]{:S(2)}, u32[]{:S(2)}) %all-to-all-start.2) | async-done | bytes 4816928 | tf_op jit(solution)/shard_map/all_to_all | solution.py:58
  210.5 0.9 slice.14
  211.5 0.1 copy.56
  211.5 0.2 fusion.2
  211.7 0.1 select_reduce_fusion.1
  211.9 0.1 copy.58
  212.0 0.7 sub.21.bidx_ref
  212.7 0.0 copy-done.3
  212.7 12.3 %shard_map.46 = bf16[8,24,64,64]{3,2,1,0:T(8,128)(2,1)} custom-call(s32[24]{0:T(128)} %copy-done.3, s32[1152]{0:T(1024)} %sub.21.bidx_ref, bf16[8,6,64,128]{3,2,1,0:T(8,128)(2,1)} %bitcast.96, bf16[48,392,128]{2,1,0:T(8,128)(2,1)} %bitcast.15.recv_ref), custom_call_target="tpu_custom_call" | custom-call | tf_op jit(solution)/shard_map/pallas_call | solution.py:98
  225.0 5.2 %reshape.223 = bf16[1,8,24,4096]{3,2,1,0:T(8,128)(2,1)} reshape(bf16[8,24,64,64]{3,2,1,0:T(8,128)(2,1)} %shard_map.46) | data formatting | bytes 3145728 | tf_op jit(solution)/shard_map/reshape | solution.py:70
  (17 shorter events, 0.2 us)
Async XLA Ops:
  6.5 82.9 %all-gather.2.cloned.1.call-start = ((), (), s32[]{:S(2)}) async-start(), calls=%async_computation.3 | async-start | bytes 4456448 | tf_op jit(solution)/shard_map/all_gather | solution.py:24
  93.9 12.7 %copy-start.1 = (s32[1,16,24]{2,1,0:T(8,128)S(1)}, s32[1,16,24]{2,1,0:T(8,128)}, u32[]{:S(2)}) copy-start(s32[1,16,24]{2,1,0:T(8,128)} %param.7) | copy-start | bytes 4612
  94.0 13.7 %copy-start.2 = (s32[1,8,6]{1,0,2:T(1,128)S(1)}, s32[1,8,6]{1,0,2:T(1,128)}, u32[]{:S(2)}) copy-start(s32[1,8,6]{1,0,2:T(1,128)} %param.6) | copy-start | bytes 580
  97.8 37.0 %all-to-all-start.1 = ((bf16[16,2,12288]{2,1,0:T(2,128)(2,1)}), bf16[16,2,12288]{2,1,0:T(2,128)(2,1)S(1)}, u32[]{:S(2)}, u32[]{:S(2)}) async-start(bf16[16,2,12288]{2,1,0:T(2,128)(2,1)} %reshape.233), calls=%async_computation.1 | async-start | bytes 1572864 | tf_op jit(solution)/shard_map/all_to_all | solution.py:28
  136.7 3.8 %copy-start = (bf16[8,64,6,128]{3,1,2,0:T(8,128)(2,1)}, bf16[8,64,6,128]{3,1,2,0:T(8,128)(2,1)S(1)}, u32[]{:S(2)}) copy-start(bf16[8,64,6,128]{3,1,2,0:T(8,128)(2,1)S(1)} %copy.50) | copy-start | bytes 2359300
  140.6 70.0 %all-to-all-start.2 = ((bf16[16,3,392,128]{3,2,1,0:T(8,128)(2,1)}), bf16[16,3,392,128]{3,2,1,0:T(8,128)(2,1)}, u32[]{:S(2)}, u32[]{:S(2)}) async-start(bf16[16,3,392,128]{3,2,1,0:T(8,128)(2,1)} %bitcast.92), calls=%async_computation.2 | async-start | bytes 9633792 | tf_op jit(solution)/shard_map/all_to_all | solution.py:58
  147.8 64.9 %copy-start.3 = (s32[24]{0:T(128)}, s32[24]{0:T(128)S(1)}, u32[]{:S(2)}) copy-start(s32[24]{0:T(128)S(1)} %add_bitcast_fusion.slot_ref) | copy-start | bytes 292
Sparse Core Ops, SparseCore 0:
  9.4 79.9 all-gather.1

commit v8 on v7

--- a/solution.py
+++ b/solution.py
@@ -71,7 +71,7 @@
 
 
 def make_pair_call(npb):
-    def pair_kernel(slot_ref, bidx_ref, own_ref, recv_ref, out_ref, al_ref):
+    def pair_kernel(slot_ref, bidx_ref, own_ref, recv_ref, out_ref, al_ref, res_ref):
         g = pl.program_id(0)
         n_loc, nblk, nosv, _ = own_ref.shape
         for j in range(npb):
@@ -89,7 +89,11 @@
             res = lax.dot_general(
                 al_ref[j], part, (((1,), (1,)), ((), ())), preferred_element_type=jnp.float32
             )
-            out_ref[:, j] = res.reshape(n_loc, nosv, nosv).astype(out_ref.dtype)
+            res_ref[j] = res
+            even = res_ref[j, pl.ds(0, n_loc * nosv // 2, stride=2), :]
+            odd = res_ref[j, pl.ds(1, n_loc * nosv // 2, stride=2), :]
+            both = jnp.concatenate([even, odd], axis=1)
+            out_ref[:, j] = both.reshape(n_loc, nosv // 2, 2 * nosv).astype(out_ref.dtype)
 
     def pair_call(slot, bidx, own_bm, recv):
         n_loc, nblk, nosv, _ = own_bm.shape
@@ -97,7 +101,7 @@
         nslot, rows, _ = recv.shape
         return pl.pallas_call(
             pair_kernel,
-            out_shape=jax.ShapeDtypeStruct((n_loc, npart, nosv, nosv), jnp.bfloat16),
+            out_shape=jax.ShapeDtypeStruct((n_loc, npart, nosv // 2, 2 * nosv), jnp.bfloat16),
             grid_spec=pltpu.PrefetchScalarGridSpec(
                 num_scalar_prefetch=2,
                 grid=(npart // npb,),
@@ -105,8 +109,11 @@
                     pl.BlockSpec((n_loc, nblk, nosv, BLK), lambda g, s, b: (0, 0, 0, 0)),
                     pl.BlockSpec((nslot, rows, BLK), lambda g, s, b: (0, 0, 0)),
                 ],
-                out_specs=pl.BlockSpec((n_loc, npb, nosv, nosv), lambda g, s, b: (0, g, 0, 0)),
-                scratch_shapes=[pltpu.VMEM((npb, n_loc * nosv, nblk * BLK), jnp.bfloat16)],
+                out_specs=pl.BlockSpec((n_loc, npb, nosv // 2, 2 * nosv), lambda g, s, b: (0, g, 0, 0)),
+                scratch_shapes=[
+                    pltpu.VMEM((npb, n_loc * nosv, nblk * BLK), jnp.bfloat16),
+                    pltpu.VMEM((npb, n_loc * nosv, nosv), jnp.float32),
+                ],
             ),
         )(slot, bidx, own_bm, recv)
 

time: 238 us -> 237 us (level)
  no operation moved by 1% of the time
where the time goes in v8:
time: 237 us; the launch traced here: 236 us
  waiting for transfers between devices  163 us (69%)
  local copies, waits for them, and re-layouts  17.9 us (8%)
  starting transfers between devices  16 us (7%)
  between operations  13.6 us (6%)
  Pallas kernels  12.9 us (5%)
  blocking collectives  6.26 us (3%)
  matrix products  4.75 us (2%)
    all_gather x1, waiting for transfers between devices, per_device(): coef = lax.all_gather(osv_coef[0], 'z', axis=0, tiled=False)  73.4 us
    all_to_all x1, waiting for transfers between devices, per_device(): recv = lax.all_to_all(send, 'orb', split_axis=0, concat_axis=0, tiled=True)  62.6 us
    all_to_all x1, waiting for transfers between devices, per_device(): lax.all_to_all(part, 'z', split_axis=0, concat_axis=3, tiled=True)[0]  26.8 us
    pallas_call x1, Pallas kernels, pair_call(): pl.pallas_call(pair_kernel, out_shape=jax.ShapeDtypeStruct((n_loc, npart,...  12.9 us
    all_to_all x1, starting transfers between devices, per_device(): lax.all_to_all(part, 'z', split_axis=0, concat_axis=3, tiled=True)[0]  8.77 us
    all_to_all x1, starting transfers between devices, per_device(): recv = lax.all_to_all(send, 'orb', split_axis=0, concat_axis=0, tiled=True)  7.23 us
    all_to_all x1, blocking collectives, per_device(): mine = lax.all_to_all(rows, 'core', split_axis=1, concat_axis=3, tiled=True)  6.26 us
    unnamed x11, local copies, waits for them, and re-layouts  4.95 us
  transfers between devices with their start and end apart: 3, of which 3 were waited for; matrix products, arithmetic and copies ran while one was open for 2% of the time, Pallas kernels for 0%

profile of v8, /device:TPU:116, one launch (start us, length us, event | category | flops | bytes accessed | tf_op | source)
XLA Modules:
  0.0 236.0 jit_solution(1785735773562151081)
XLA Ops:
  6.5 0.0 all-gather.2.cloned.1.call-start
  6.5 0.7 all-gather.2.cloned.1.call-update
  7.3 2.2 copy.47
  9.5 6.3 %all_to_all.35 = bf16[16,2,8,24,256]{4,3,2,0,1:T(8,128)(2,1)S(1)} all-to-all(bf16[16,2,8,24,256]{4,3,2,0,1:T(8,128)(2,1)S(1)} %copy.47), channel_id=1, replica_groups=mesh['z'=16,'core'=2,'orb'=16] {'core'}, dimensions={1} | all-to-all | bytes 6291456 | tf_op jit(solution)/shard_map/all_to_all | solution.py:22
  15.7 0.3 copy.48
  16.0 73.4 %all-gather.2.cloned.1.call-done = bf16[16,8,256,64]{2,3,1,0:T(8,128)(2,1)} async-done(((bf16[1,8,256,64]{2,3,1,0:T(8,128)(2,1)}), bf16[16,8,256,64]{2,3,1,0:T(8,128)(2,1)}) %all-gather.2.cloned.1.call-update) | async-done | bytes 4194320 | tf_op jit(solution)/shard_map/all_gather | solution.py:24
  89.4 4.6 %fusion.16 = bf16[16,8,48,64]{3,2,1,0:T(8,128)(2,1)} fusion(bf16[16,8,256,64]{2,3,1,0:T(8,128)(2,1)} %all-gather.2.cloned.1.call-done, bf16[16,8,48,256]{3,2,1,0:T(8,128)(2,1)S(1)} %bitcast.93), kind=kOutput, calls=%fused_computation.51 | convolution fusion | flops 201719808 | bytes 8126464 | tf_op jit(solution)/shard_map/zkfm,zkma->zkaf/dot_general | solution.py:25
  93.9 0.0 copy-start.1
  94.0 0.0 copy-start.2
  94.0 3.9 %reshape.233 = bf16[16,2,12288]{2,1,0:T(2,128)(2,1)} reshape(bf16[16,8,48,64]{3,2,1,0:T(8,128)(2,1)} %fusion.16) | data formatting | bytes 1572864
  97.8 8.8 %all-to-all-start.1 = ((bf16[16,2,12288]{2,1,0:T(2,128)(2,1)}), bf16[16,2,12288]{2,1,0:T(2,128)(2,1)S(1)}, u32[]{:S(2)}, u32[]{:S(2)}) async-start(bf16[16,2,12288]{2,1,0:T(2,128)(2,1)} %reshape.233), calls=%async_computation.1 | async-start | bytes 1572864 | tf_op jit(solution)/shard_map/all_to_all | solution.py:28
  106.6 0.1 fusion.1
  106.7 0.0 copy-done.1
  106.7 0.4 select_reduce_fusion
  107.2 0.1 convert_reduce_fusion
  107.3 0.1 copy.54
  107.4 0.1 copy.55
  107.5 0.1 reshape.226
  107.6 0.0 copy-done.2
  107.6 0.1 copy.51
  107.8 0.1 pad.3.clone
  107.8 0.1 pad.4.clone
  107.9 26.8 %all-to-all-done.1 = bf16[16,2,12288]{2,1,0:T(2,128)(2,1)S(1)} async-done(((bf16[16,2,12288]{2,1,0:T(2,128)(2,1)}), bf16[16,2,12288]{2,1,0:T(2,128)(2,1)S(1)}, u32[]{:S(2)}, u32[]{:S(2)}) %all-to-all-start.1) | async-done | bytes 786464 | tf_op jit(solution)/shard_map/all_to_all | solution.py:28
  134.8 1.0 reshape.234
  135.8 0.1 bitcast_bitcast_fusion
  135.9 0.1 copy.49
  136.0 0.7 copy.50
  136.7 0.0 copy-start
  136.8 0.2 maximum_maximum_fusion
  137.0 3.6 %gather_fusion = bf16[48,392,128]{2,1,0:T(8,128)(2,1)} fusion(bf16[8,392,128]{2,1,0:T(8,128)(2,1)S(1)} %maximum_maximum_fusion, s32[1024]{0:T(1024)S(1)} %pad_clamp_fusion), kind=kCustom, calls=%fused_computation | custom fusion | bytes 9633984 | tf_op jit(solution)/shard_map/jit(_take)/gather | solution.py:57
  140.6 0.0 copy-done
  140.6 7.2 %all-to-all-start.2 = ((bf16[16,3,392,128]{3,2,1,0:T(8,128)(2,1)}), bf16[16,3,392,128]{3,2,1,0:T(8,128)(2,1)}, u32[]{:S(2)}, u32[]{:S(2)}) async-start(bf16[16,3,392,128]{3,2,1,0:T(8,128)(2,1)} %bitcast.92), calls=%async_computation.2 | async-start | bytes 9633792 | tf_op jit(solution)/shard_map/all_to_all | solution.py:58
  147.8 0.0 copy-start.3
  147.9 62.6 %all-to-all-done.2 = bf16[16,3,392,128]{3,2,1,0:T(8,128)(2,1)} async-done(((bf16[16,3,392,128]{3,2,1,0:T(8,128)(2,1)}), bf16[16,3,392,128]{3,2,1,0:T(8,128)(2,1)}, u32[]{:S(2)}, u32[]{:S(2)}) %all-to-all-start.2) | async-done | bytes 4816928 | tf_op jit(solution)/shard_map/all_to_all | solution.py:58
  210.4 0.9 slice.14
  211.3 0.1 copy.56
  211.4 0.2 fusion.2
  211.6 0.1 select_reduce_fusion.1
  211.7 0.1 copy.58
  211.9 0.7 sub.21.bidx_ref
  212.6 0.0 copy-done.3
  212.6 12.9 %shard_map.46 = bf16[8,24,32,128]{3,2,1,0:T(8,128)(2,1)} custom-call(s32[24]{0:T(128)} %copy-done.3, s32[1152]{0:T(1024)} %sub.21.bidx_ref, bf16[8,6,64,128]{3,2,1,0:T(8,128)(2,1)} %bitcast.96, bf16[48,392,128]{2,1,0:T(8,128)(2,1)} %bitcast.15.recv_ref), custom_call_target="tpu_custom_call" | custom-call | tf_op jit(solution)/shard_map/pallas_call | solution.py:102
  225.5 3.7 %reshape.223 = bf16[1,8,24,4096]{3,2,1,0:T(8,128)(2,1)} reshape(bf16[8,24,32,128]{3,2,1,0:T(8,128)(2,1)} %shard_map.46) | data formatting | bytes 3145728 | tf_op jit(solution)/shard_map/reshape | solution.py:70
  (17 shorter events, 0.2 us)
Async XLA Ops:
  6.5 82.9 %all-gather.2.cloned.1.call-start = ((), (), s32[]{:S(2)}) async-start(), calls=%async_computation.3 | async-start | bytes 4456448 | tf_op jit(solution)/shard_map/all_gather | solution.py:24
  93.9 12.7 %copy-start.1 = (s32[1,16,24]{2,1,0:T(8,128)S(1)}, s32[1,16,24]{2,1,0:T(8,128)}, u32[]{:S(2)}) copy-start(s32[1,16,24]{2,1,0:T(8,128)} %param.7) | copy-start | bytes 4612
  94.0 13.7 %copy-start.2 = (s32[1,8,6]{1,0,2:T(1,128)S(1)}, s32[1,8,6]{1,0,2:T(1,128)}, u32[]{:S(2)}) copy-start(s32[1,8,6]{1,0,2:T(1,128)} %param.6) | copy-start | bytes 580
  97.8 37.0 %all-to-all-start.1 = ((bf16[16,2,12288]{2,1,0:T(2,128)(2,1)}), bf16[16,2,12288]{2,1,0:T(2,128)(2,1)S(1)}, u32[]{:S(2)}, u32[]{:S(2)}) async-start(bf16[16,2,12288]{2,1,0:T(2,128)(2,1)} %reshape.233), calls=%async_computation.1 | async-start | bytes 1572864 | tf_op jit(solution)/shard_map/all_to_all | solution.py:28
  136.7 3.8 %copy-start = (bf16[8,64,6,128]{3,1,2,0:T(8,128)(2,1)}, bf16[8,64,6,128]{3,1,2,0:T(8,128)(2,1)S(1)}, u32[]{:S(2)}) copy-start(bf16[8,64,6,128]{3,1,2,0:T(8,128)(2,1)S(1)} %copy.50) | copy-start | bytes 2359300
  140.6 69.8 %all-to-all-start.2 = ((bf16[16,3,392,128]{3,2,1,0:T(8,128)(2,1)}), bf16[16,3,392,128]{3,2,1,0:T(8,128)(2,1)}, u32[]{:S(2)}, u32[]{:S(2)}) async-start(bf16[16,3,392,128]{3,2,1,0:T(8,128)(2,1)} %bitcast.92), calls=%async_computation.2 | async-start | bytes 9633792 | tf_op jit(solution)/shard_map/all_to_all | solution.py:58
  147.8 64.8 %copy-start.3 = (s32[24]{0:T(128)}, s32[24]{0:T(128)S(1)}, u32[]{:S(2)}) copy-start(s32[24]{0:T(128)S(1)} %add_bitcast_fusion.slot_ref) | copy-start | bytes 292
Sparse Core Ops, SparseCore 0:
  9.4 79.9 all-gather.1

commit v9 on v8

--- a/solution.py
+++ b/solution.py
@@ -66,7 +66,9 @@
     pblocks = (pcode[:, :FBLK] * 8 + pcode[:, FBLK:]).astype(jnp.int32)
     match = pblocks[:, None, None, :] == own_blocks[None, :, :, None]
     bidx = jnp.sum(jnp.where(match, jnp.arange(1, FBLK + 1)[None, None, :, None], 0), axis=2) - 1
-    pair = pair_call(slot, bidx.astype(jnp.int32).reshape(-1), blocks_major, recv)
+    bidx = jnp.where(bidx < 0, FBLK, bidx)
+    own_pad = jnp.concatenate([blocks_major, jnp.zeros_like(blocks_major[:, :1])], axis=1)
+    pair = pair_call(slot, bidx.astype(jnp.int32).reshape(-1), own_pad, recv)
     return pair.reshape(1, n_loc, npart, nosv * nosv)
 
 
@@ -74,14 +76,14 @@
     def pair_kernel(slot_ref, bidx_ref, own_ref, recv_ref, out_ref, al_ref, res_ref):
         g = pl.program_id(0)
         n_loc, nblk, nosv, _ = own_ref.shape
+        nblk -= 1
         for j in range(npb):
             n = g * npb + j
             s = slot_ref[n]
             for r in range(n_loc):
                 for e in range(nblk):
                     b = bidx_ref[(n * n_loc + r) * nblk + e]
-                    blk = own_ref[r, jnp.maximum(b, 0)]
-                    blk = jnp.where(b >= 0, blk, jnp.zeros_like(blk))
+                    blk = own_ref[r, b]
                     al_ref[j, r * nosv : (r + 1) * nosv, e * BLK : (e + 1) * BLK] = blk
             part = jnp.concatenate(
                 [recv_ref[s, e * nosv : (e + 1) * nosv, :] for e in range(nblk)], axis=1
@@ -106,12 +108,12 @@
                 num_scalar_prefetch=2,
                 grid=(npart // npb,),
                 in_specs=[
-                    pl.BlockSpec((n_loc, nblk, nosv, BLK), lambda g, s, b: (0, 0, 0, 0)),
+                    pl.BlockSpec(own_bm.shape, lambda g, s, b: (0, 0, 0, 0)),
                     pl.BlockSpec((nslot, rows, BLK), lambda g, s, b: (0, 0, 0)),
                 ],
                 out_specs=pl.BlockSpec((n_loc, npb, nosv // 2, 2 * nosv), lambda g, s, b: (0, g, 0, 0)),
                 scratch_shapes=[
-                    pltpu.VMEM((npb, n_loc * nosv, nblk * BLK), jnp.bfloat16),
+                    pltpu.VMEM((npb, n_loc * nosv, (nblk - 1) * BLK), jnp.bfloat16),
                     pltpu.VMEM((npb, n_loc * nosv, nosv), jnp.float32),
                 ],
             ),
@@ -120,7 +122,7 @@
     return pair_call
 
 
-pair_call = make_pair_call(4)
+pair_call = make_pair_call(8)
 
 
 def solution(mesh):

time: 237 us -> 235 us (level)
    unnamed x11 -> x9, local copies, waits for them, and re-layouts: 4.95 us -> 4.96 us
where the time goes in v9:
time: 235 us; the launch traced here: 234 us
  waiting for transfers between devices  163 us (69%)
  local copies, waits for them, and re-layouts  18.4 us (8%)
  starting transfers between devices  16 us (7%)
  between operations  13.6 us (6%)
  Pallas kernels  10.7 us (5%)
  blocking collectives  6.26 us (3%)
  matrix products  4.75 us (2%)
    all_gather x1, waiting for transfers between devices, per_device(): coef = lax.all_gather(osv_coef[0], 'z', axis=0, tiled=False)  73.4 us
    all_to_all x1, waiting for transfers between devices, per_device(): recv = lax.all_to_all(send, 'orb', split_axis=0, concat_axis=0, tiled=True)  61.7 us
    all_to_all x1, waiting for transfers between devices, per_device(): lax.all_to_all(part, 'z', split_axis=0, concat_axis=3, tiled=True)[0]  26.8 us
    pallas_call x1, Pallas kernels, pair_call(): pl.pallas_call(pair_kernel, out_shape=jax.ShapeDtypeStruct((n_loc, npart,...  10.7 us
    all_to_all x1, starting transfers between devices, per_device(): lax.all_to_all(part, 'z', split_axis=0, concat_axis=3, tiled=True)[0]  8.77 us
    all_to_all x1, starting transfers between devices, per_device(): recv = lax.all_to_all(send, 'orb', split_axis=0, concat_axis=0, tiled=True)  7.23 us
    all_to_all x1, blocking collectives, per_device(): mine = lax.all_to_all(rows, 'core', split_axis=1, concat_axis=3, tiled=True)  6.26 us
    unnamed x9, local copies, waits for them, and re-layouts  4.96 us
  transfers between devices with their start and end apart: 3, of which 3 were waited for; matrix products, arithmetic and copies ran while one was open for 2% of the time, Pallas kernels for 0%

profile of v9, /device:TPU:116, one launch (start us, length us, event | category | flops | bytes accessed | tf_op | source)
XLA Modules:
  0.0 234.1 jit_solution(2479961118252258482)
XLA Ops:
  6.5 0.0 all-gather.2.cloned.1.call-start
  6.5 0.7 all-gather.2.cloned.1.call-update
  7.3 2.2 copy.47
  9.5 6.3 %all_to_all.35 = bf16[16,2,8,24,256]{4,3,2,0,1:T(8,128)(2,1)S(1)} all-to-all(bf16[16,2,8,24,256]{4,3,2,0,1:T(8,128)(2,1)S(1)} %copy.47), channel_id=1, replica_groups=mesh['z'=16,'core'=2,'orb'=16] {'core'}, dimensions={1} | all-to-all | bytes 6291456 | tf_op jit(solution)/shard_map/all_to_all | solution.py:22
  15.7 0.3 copy.48
  16.0 73.4 %all-gather.2.cloned.1.call-done = bf16[16,8,256,64]{2,3,1,0:T(8,128)(2,1)} async-done(((bf16[1,8,256,64]{2,3,1,0:T(8,128)(2,1)}), bf16[16,8,256,64]{2,3,1,0:T(8,128)(2,1)}) %all-gather.2.cloned.1.call-update) | async-done | bytes 4194320 | tf_op jit(solution)/shard_map/all_gather | solution.py:24
  89.4 4.6 %fusion.16 = bf16[16,8,48,64]{3,2,1,0:T(8,128)(2,1)} fusion(bf16[16,8,256,64]{2,3,1,0:T(8,128)(2,1)} %all-gather.2.cloned.1.call-done, bf16[16,8,48,256]{3,2,1,0:T(8,128)(2,1)S(1)} %bitcast.93), kind=kOutput, calls=%fused_computation.52 | convolution fusion | flops 201719808 | bytes 8126464 | tf_op jit(solution)/shard_map/zkfm,zkma->zkaf/dot_general | solution.py:25
  93.9 0.0 copy-start
  94.0 0.0 copy-start.1
  94.0 3.9 %reshape.233 = bf16[16,2,12288]{2,1,0:T(2,128)(2,1)} reshape(bf16[16,8,48,64]{3,2,1,0:T(8,128)(2,1)} %fusion.16) | data formatting | bytes 1572864
  97.8 8.8 %all-to-all-start.1 = ((bf16[16,2,12288]{2,1,0:T(2,128)(2,1)}), bf16[16,2,12288]{2,1,0:T(2,128)(2,1)S(1)}, u32[]{:S(2)}, u32[]{:S(2)}) async-start(bf16[16,2,12288]{2,1,0:T(2,128)(2,1)} %reshape.233), calls=%async_computation.1 | async-start | bytes 1572864 | tf_op jit(solution)/shard_map/all_to_all | solution.py:28
  106.6 0.1 fusion.1
  106.7 0.0 copy-done
  106.7 0.4 select_reduce_fusion
  107.2 0.1 convert_reduce_fusion
  107.3 0.1 copy.54
  107.5 0.1 copy.55
  107.5 0.1 reshape.226
  107.6 0.0 copy-done.1
  107.7 0.1 copy.51
  107.8 0.1 pad.4.clone
  107.9 0.1 pad.5.clone
  107.9 26.8 %all-to-all-done.1 = bf16[16,2,12288]{2,1,0:T(2,128)(2,1)S(1)} async-done(((bf16[16,2,12288]{2,1,0:T(2,128)(2,1)}), bf16[16,2,12288]{2,1,0:T(2,128)(2,1)S(1)}, u32[]{:S(2)}, u32[]{:S(2)}) %all-to-all-start.1) | async-done | bytes 786464 | tf_op jit(solution)/shard_map/all_to_all | solution.py:28
  134.8 1.0 reshape.234
  135.8 0.1 bitcast_bitcast_fusion
  135.9 0.1 copy.49
  136.0 0.7 copy.50
  136.8 0.2 maximum_maximum_fusion
  137.0 3.6 %gather_fusion = bf16[48,392,128]{2,1,0:T(8,128)(2,1)} fusion(bf16[8,392,128]{2,1,0:T(8,128)(2,1)S(1)} %maximum_maximum_fusion, s32[1024]{0:T(1024)S(1)} %pad_clamp_fusion), kind=kCustom, calls=%fused_computation | custom fusion | bytes 9633984 | tf_op jit(solution)/shard_map/jit(_take)/gather | solution.py:57
  140.6 7.2 %all-to-all-start.2 = ((bf16[16,3,392,128]{3,2,1,0:T(8,128)(2,1)}), bf16[16,3,392,128]{3,2,1,0:T(8,128)(2,1)}, u32[]{:S(2)}, u32[]{:S(2)}) async-start(bf16[16,3,392,128]{3,2,1,0:T(8,128)(2,1)} %bitcast.92), calls=%async_computation.2 | async-start | bytes 9633792 | tf_op jit(solution)/shard_map/all_to_all | solution.py:58
  147.8 0.0 copy-start.2
  147.8 1.0 concatenate.25.own_ref
  148.9 61.7 %all-to-all-done.2 = bf16[16,3,392,128]{3,2,1,0:T(8,128)(2,1)} async-done(((bf16[16,3,392,128]{3,2,1,0:T(8,128)(2,1)}), bf16[16,3,392,128]{3,2,1,0:T(8,128)(2,1)}, u32[]{:S(2)}, u32[]{:S(2)}) %all-to-all-start.2) | async-done | bytes 4816928 | tf_op jit(solution)/shard_map/all_to_all | solution.py:58
  210.6 0.9 slice.14
  211.5 0.1 copy.56
  211.6 0.2 fusion.2
  211.8 0.1 select_reduce_fusion.1
  211.9 0.1 copy.58
  212.1 0.1 sub.21
  212.2 0.6 compare_select_fusion.bidx_ref
  212.8 0.0 copy-done.2
  212.8 10.7 %shard_map.46 = bf16[8,24,32,128]{3,2,1,0:T(8,128)(2,1)} custom-call(s32[24]{0:T(128)} %copy-done.2, s32[1152]{0:T(1024)} %compare_select_fusion.bidx_ref, bf16[8,7,64,128]{3,2,1,0:T(8,128)(2,1)} %concatenate.25.own_ref, bf16[48,392,128]{2,1,0:T(8,128)(2,1)} %bitcast.15.recv_ref), custom_call_target="tpu_custom_call" | custom-call | tf_op jit(solution)/shard_map/pallas_call | solution.py:104
  223.5 3.7 %reshape.223 = bf16[1,8,24,4096]{3,2,1,0:T(8,128)(2,1)} reshape(bf16[8,24,32,128]{3,2,1,0:T(8,128)(2,1)} %shard_map.46) | data formatting | bytes 3145728 | tf_op jit(solution)/shard_map/reshape | solution.py:72
  (17 shorter events, 0.2 us)
Async XLA Ops:
  6.5 82.9 %all-gather.2.cloned.1.call-start = ((), (), s32[]{:S(2)}) async-start(), calls=%async_computation.3 | async-start | bytes 4456448 | tf_op jit(solution)/shard_map/all_gather | solution.py:24
  93.9 12.7 %copy-start = (s32[1,16,24]{2,1,0:T(8,128)S(1)}, s32[1,16,24]{2,1,0:T(8,128)}, u32[]{:S(2)}) copy-start(s32[1,16,24]{2,1,0:T(8,128)} %param.7) | copy-start | bytes 4612
  94.0 13.7 %copy-start.1 = (s32[1,8,6]{1,0,2:T(1,128)S(1)}, s32[1,8,6]{1,0,2:T(1,128)}, u32[]{:S(2)}) copy-start(s32[1,8,6]{1,0,2:T(1,128)} %param.6) | copy-start | bytes 580
  97.8 37.0 %all-to-all-start.1 = ((bf16[16,2,12288]{2,1,0:T(2,128)(2,1)}), bf16[16,2,12288]{2,1,0:T(2,128)(2,1)S(1)}, u32[]{:S(2)}, u32[]{:S(2)}) async-start(bf16[16,2,12288]{2,1,0:T(2,128)(2,1)} %reshape.233), calls=%async_computation.1 | async-start | bytes 1572864 | tf_op jit(solution)/shard_map/all_to_all | solution.py:28
  140.6 70.0 %all-to-all-start.2 = ((bf16[16,3,392,128]{3,2,1,0:T(8,128)(2,1)}), bf16[16,3,392,128]{3,2,1,0:T(8,128)(2,1)}, u32[]{:S(2)}, u32[]{:S(2)}) async-start(bf16[16,3,392,128]{3,2,1,0:T(8,128)(2,1)} %bitcast.92), calls=%async_computation.2 | async-start | bytes 9633792 | tf_op jit(solution)/shard_map/all_to_all | solution.py:58
  147.8 65.0 %copy-start.2 = (s32[24]{0:T(128)}, s32[24]{0:T(128)S(1)}, u32[]{:S(2)}) copy-start(s32[24]{0:T(128)S(1)} %add_bitcast_fusion.slot_ref) | copy-start | bytes 292
Sparse Core Ops, SparseCore 0:
  9.4 79.9 all-gather.1
